TPU v7x, 512 devices: a whole 4x8x8 slice. The times are simulated.
512 devices in a mesh: row: 64 (over y, x, core), col: 8 (over z).
Axes of the slice: x: 4, y: 8, z: 8, core: 2. Of those that a mesh axis runs over, the one named last changes fastest.
Arguments:
- panel_cols: float32 [16384, 256], P('row'), may hold values from -60 to 60, as said below
- affinity: float32 [16384, 16384], P('row', 'col'), may hold values from -8 to 8, as said below
Outputs:
- updated: float32 [16384, 16384], P('row', 'col')
- band_block: float32 [256, 256], replicated
Inputs may be any that keep to these rules, and one draw needn't show every extreme that they name: affinity holds a symmetric matrix in the stored column order of the steps. panel_cols has full column rank.
All inputs are finite; a program needn't handle non-finite values.
Results may differ from a plain program's by a relative error of at most 0.000071.
Values sent between devices are 32-bit elements; how exact they have to be, the bound alone decides.
No kernel may reach another device: no remote copies, remote signals or barrier semaphores. Data moves between devices by JAX's collectives and lax.ppermute only.
A program may use at most 64 MiB of HBM per device.

v0:
```python
import jax
import jax.numpy as jnp
from jax import lax
from jax.sharding import PartitionSpec as P


def shards(panel_cols, affinity):
    high = lax.Precision.HIGHEST
    local_rows = panel_cols.shape[0]
    piece_rows = local_rows // lax.axis_size("col")
    col_place = lax.axis_index("col")
    gram_sum = lax.psum(jnp.dot(panel_cols.T, panel_cols, precision=high), "row")
    lower_factor = jnp.linalg.cholesky(gram_sum)
    ortho_basis = jax.scipy.linalg.solve_triangular(lower_factor, panel_cols.T, lower=True).T
    own_basis = lax.dynamic_slice_in_dim(ortho_basis, col_place * piece_rows, piece_rows, 0)
    arrived = lax.all_gather(own_basis, "row", axis=0, tiled=True)
    partial_sum = jnp.dot(affinity, arrived, precision=high)
    partial_sum, basis_cols = (partial_sum, arrived)
    moment = lax.psum(partial_sum, "col")
    band_block = lax.psum(jnp.dot(ortho_basis.T, moment, precision=high), "row")
    corrected = moment - 0.5 * jnp.dot(ortho_basis, band_block, precision=high)
    own_corrected = lax.dynamic_slice_in_dim(corrected, col_place * piece_rows, piece_rows, 0)
    update_cols = lax.all_gather(own_corrected, "row", axis=0, tiled=True)
    updated = affinity - jnp.dot(ortho_basis, update_cols.T, precision=high)
    updated = updated - jnp.dot(corrected, basis_cols.T, precision=high)
    return (updated, band_block)


def solution(mesh):
    placed = (P("row", None), P("row", "col"))
    return jax.shard_map(
        shards, mesh=mesh, in_specs=placed, out_specs=(P("row", "col"), P()), check_vma=False
    )
```

profile of v0, /device:TPU:1, one launch (start us, length us, event | category | flops | bytes accessed | tf_op | source)
XLA Modules:
  0.0 722.9 jit_solution(2886932835697183772)
XLA Ops:
  7.2 2.3 fusion.16
  9.6 196.8 %all-reduce.5.cloned.1.call-done = f32[256,256]{0,1:T(8,128)} async-done(((f32[256,256]{0,1:T(8,128)}), f32[256,256]{0,1:T(8,128)}) %all-reduce.5.cloned.1.call-update) | async-done | bytes 262160 | tf_op jit(solution)/shard_map/psum | solution.py:12
  206.4 1.1 copy.8
  207.5 1.0 fusion.1
  208.5 11.7 %cholesky.50 = f32[128,128]{1,0:T(8,128)S(1)} custom-call(f32[128,128]{1,0:T(8,128)S(1)} %cholesky.118), custom_call_target="Cholesky" | custom-call | tf_op jit(solution)/shard_map/jit(cholesky)/cholesky | solution.py:13
  220.3 9.8 %custom-call.15 = f32[1,128,128]{1,2,0:T(8,128)S(1)} custom-call(f32[1,128,128]{2,1,0:T(8,128)S(1)} %get-tuple-element.23), custom_call_target="InvertDiagBlocksLowerTriangular" | custom-call | tf_op jit(solution)/shard_map/jit(cholesky)/cholesky | solution.py:13
  230.6 11.7 %cholesky.105 = f32[128,128]{1,0:T(8,128)S(1)} custom-call(f32[128,128]{1,0:T(8,128)S(1)} %convolution_subtract_fusion.3), custom_call_target="Cholesky" | custom-call | tf_op jit(solution)/shard_map/jit(cholesky)/cholesky | solution.py:13
  242.3 0.7 compare_reduce_fusion
  244.4 4.1 while.1
  245.1 1.4 bitcast_dynamic-update-slice_fusion.2
  247.1 1.4 bitcast_dynamic-update-slice_fusion.2
  248.5 19.7 %custom-call.16 = f32[2,128,128]{1,2,0:T(8,128)S(1)} custom-call(f32[2,128,128]{2,1,0:T(8,128)S(1)} %get-tuple-element.9), custom_call_target="InvertDiagBlocksLowerTriangular" | custom-call | tf_op jit(solution)/shard_map/jit(_solve_triangular)/triangular_solve | solution.py:14
  269.3 0.7 copy.9
  270.1 80.7 %all-gather.3.cloned.1.call-done = f32[2048,256]{1,0:T(8,128)} async-done(((f32[32,256]{1,0:T(8,128)}), f32[2048,256]{1,0:T(8,128)}) %all-gather.3.cloned.1.call-update) | async-done | bytes 2097168 | tf_op jit(solution)/shard_map/all_gather | solution.py:16
  350.7 4.2 convolution_bitcast_fusion
  355.0 71.6 %all-reduce.7.cloned.1.call-done = f32[256,256]{1,0:T(8,128)} async-done(((f32[256,256]{1,0:T(8,128)}), f32[256,256]{1,0:T(8,128)}) %all-reduce.7.cloned.1.call-update) | async-done | bytes 262160 | tf_op jit(solution)/shard_map/psum | solution.py:19
  426.6 2.0 fusion.2
  428.7 193.9 %all-reduce.9.cloned.1.call-done = f32[256,256]{1,0:T(8,128)} async-done(((f32[256,256]{1,0:T(8,128)}), f32[256,256]{1,0:T(8,128)}) %all-reduce.9.cloned.1.call-update) | async-done | bytes 262160 | tf_op jit(solution)/shard_map/psum | solution.py:20
  622.6 1.6 fusion
  624.2 0.6 constant_dynamic-slice_fusion.1
  624.9 82.1 %all-gather.5.cloned.1.call-done = f32[2048,256]{1,0:T(8,128)} async-done(((f32[32,256]{1,0:T(8,128)}), f32[2048,256]{1,0:T(8,128)}) %all-gather.5.cloned.1.call-update) | async-done | bytes 2097168 | tf_op jit(solution)/shard_map/all_gather | solution.py:23
  707.0 5.3 convolution_subtract_fusion.1
  712.3 3.4 convolution_subtract_fusion
  715.6 0.7 copy.26
  (36 shorter events, 3.3 us)
Async XLA Ops:
  7.2 199.3 %all-reduce.5.cloned.1.call-start = ((), (), s32[]{:S(2)}) async-start(), calls=%async_computation | async-start | bytes 524288 | tf_op jit(solution)/shard_map/psum | solution.py:12
  9.5 258.6 %copy-start.2 = (f32[256,256]{1,0:T(8,128)S(1)}, f32[256,256]{1,0:T(8,128)}, u32[]{:S(2)}) copy-start(f32[256,256]{1,0:T(8,128)} %param.2) | copy-start | bytes 786436
  9.6 341.1 %all-gather.3.cloned.1.call-start = ((), (), s32[]{:S(2)}) async-start(), calls=%async_computation.1 | async-start | bytes 2129920 | tf_op jit(solution)/shard_map/all_gather | solution.py:16
  220.2 130.5 %copy-start = (f32[256,2048]{1,0:T(8,128)S(1)}, f32[256,2048]{1,0:T(8,128)}, u32[]{:S(2)}) copy-start(f32[256,2048]{1,0:T(8,128)} %param.3) | copy-start | bytes 6291460
  270.0 156.6 %all-reduce.7.cloned.1.call-start = ((), (), s32[]{:S(2)}) async-start(), calls=%async_computation.2 | async-start | bytes 524288 | tf_op jit(solution)/shard_map/psum | solution.py:19
  355.0 267.6 %all-reduce.9.cloned.1.call-start = ((), (), s32[]{:S(2)}) async-start(), calls=%async_computation.3 | async-start | bytes 524288 | tf_op jit(solution)/shard_map/psum | solution.py:20
  428.7 278.3 %all-gather.5.cloned.1.call-start = ((), (), s32[]{:S(2)}) async-start(), calls=%async_computation.4 | async-start | bytes 2129920 | tf_op jit(solution)/shard_map/all_gather | solution.py:23
  707.0 5.3 copy-start.1
  712.2 3.4 copy-start.3
Sparse Core Ops, SparseCore 0:
  12.0 194.3 all-reduce.4
  270.1 80.5 all-gather.2
  355.1 71.4 all-reduce.6
  430.5 192.0 all-reduce.8
  626.4 80.5 all-gather.4
where the time goes:
time: 723 us
  waiting for transfers between devices  625 us (86%)
  other arithmetic  54.8 us (8%)
  matrix products  20.3 us (3%)
  between operations  15.2 us (2%)
    psum x1, waiting for transfers between devices, shards(): lax.psum(jnp.dot(panel_cols.T, panel_cols, precision=high), 'row')  197 us
    psum x1, waiting for transfers between devices, shards(): band_block = lax.psum(jnp.dot(ortho_basis.T, moment, precision=high), 'row')  194 us
    all_gather x1, waiting for transfers between devices, shards(): update_cols = lax.all_gather(own_corrected, 'row', axis=0, tiled=True)  82.1 us
    all_gather x1, waiting for transfers between devices, shards(): arrived = lax.all_gather(own_basis, 'row', axis=0, tiled=True)  80.7 us
    psum x1, waiting for transfers between devices, shards(): moment = lax.psum(partial_sum, 'col')  71.6 us
    another operation x6, other arithmetic, shards(): lower_factor = jnp.linalg.cholesky(gram_sum)  34 us
    another operation x3, other arithmetic, shards(): jax.scipy.linalg.solve_triangular(lower_factor, panel_cols.T, lower=True)  19.7 us
  transfers between devices with their start and end apart: 5, of which 5 were waited for; matrix products, arithmetic and copies ran while one was open for 0% of the time, Pallas kernels for 0%

commit v1 on v0

v1 whole, which is shorter than its diff:
```python
import jax
import jax.numpy as jnp
from jax import lax
from jax.sharding import PartitionSpec as P


def _dot(a, b):
    return jnp.dot(a, b, precision=lax.Precision.HIGHEST)


def _exchange(x, axis):
    return lax.all_to_all(x, axis, 0, 0, tiled=False)


def shards(panel_cols, affinity):
    local_rows, k = panel_cols.shape
    n_row = lax.axis_size("row")
    n_col = lax.axis_size("col")
    piece = local_rows // n_col
    col_place = lax.axis_index("col")

    gram_part = _dot(panel_cols.T, panel_cols)
    gram_rows = _exchange(gram_part.reshape(n_row, k // n_row, k), "row").sum(0)
    gram_sum = _exchange(jnp.broadcast_to(gram_rows[None], (n_row,) + gram_rows.shape), "row").reshape(k, k)

    own_panel = lax.dynamic_slice_in_dim(panel_cols, col_place * piece, piece, 0)
    panel_stored = _exchange(jnp.broadcast_to(own_panel[None], (n_row, piece, k)), "row").reshape(n_row * piece, k)

    lower_factor = jnp.linalg.cholesky(gram_sum)
    eye = jnp.eye(k, dtype=panel_cols.dtype)
    inv_lower = jax.scipy.linalg.solve_triangular(lower_factor, eye, lower=True)
    basis_own = _dot(panel_cols, inv_lower.T)
    basis_stored = _dot(panel_stored, inv_lower.T)

    partial_sum = _dot(affinity, basis_stored)
    gathered = _exchange(jnp.broadcast_to(partial_sum[None], (n_col,) + partial_sum.shape), "col")
    moment_own = gathered.sum(0)
    band_part = _dot(basis_own.T, moment_own)

    own_moment = lax.dynamic_slice_in_dim(moment_own, col_place * piece, piece, 0)
    send = jnp.concatenate(
        [
            jnp.broadcast_to(own_moment.reshape(1, piece * k), (n_row, piece * k)),
            band_part.reshape(n_row, (k // n_row) * k),
        ],
        axis=1,
    )
    got = _exchange(send, "row")
    moment_stored = got[:, : piece * k].reshape(n_row * piece, k)
    band_rows = got[:, piece * k :].sum(0)
    band_block = _exchange(jnp.broadcast_to(band_rows[None], (n_row,) + band_rows.shape), "row").reshape(k, k)

    corrected_own = moment_own - 0.5 * _dot(basis_own, band_block)
    corrected_stored = moment_stored - 0.5 * _dot(basis_stored, band_block)
    updated = affinity - _dot(basis_own, corrected_stored.T)
    updated = updated - _dot(corrected_own, basis_stored.T)
    return (updated, band_block)


def solution(mesh):
    placed = (P("row", None), P("row", "col"))
    return jax.shard_map(
        shards, mesh=mesh, in_specs=placed, out_specs=(P("row", "col"), P()), check_vma=False
    )
```

time: 723 us -> 294 us (0.41)
  waiting for transfers between devices: 625 us -> 71.7 us
  blocking collectives: 0 us -> 92.9 us
  starting transfers between devices: 0.21 us -> 24.7 us
  local copies, waits for them, and re-layouts: 7.1 us -> 20.7 us
  between operations: 15.2 us -> 2.46 us
    psum x3 -> x0, waiting for transfers between devices: 462 us -> none  [the longest x1 197 us: shards(): lax.psum(jnp.dot(panel_cols.T, panel_cols, precision=high), 'row')]
    all_gather x2 -> x0, waiting for transfers between devices: 163 us -> none  [the longest x1 82.1 us: shards(): update_cols = lax.all_gather(own_corrected, 'row', axis=0, tiled=True)]
    all_to_all x0 -> x2, blocking collectives: none -> 92.9 us  [_exchange(): return lax.all_to_all(x, axis, 0, 0, tiled=False)]
    all_to_all x0 -> x4, waiting for transfers between devices: none -> 71.7 us  [_exchange(): return lax.all_to_all(x, axis, 0, 0, tiled=False)]
    all_to_all x0 -> x4, starting transfers between devices: none -> 24.7 us  [_exchange(): return lax.all_to_all(x, axis, 0, 0, tiled=False)]
    dot_general x6 -> x9, matrix products: 18.8 us -> 19.6 us  [_dot(): return jnp.dot(a, b, precision=lax.Precision.HIGHEST)]
  transfers between devices with their start and end apart: 5 -> 4, of which waited for: 5 -> 3; matrix products, arithmetic and copies ran while one was open for 0% -> 23% of each run, Pallas kernels for 0% -> 0%
where the time goes in v1:
time: 294 us; the launch traced here: 290 us
  blocking collectives  92.9 us (32%)
  waiting for transfers between devices  71.7 us (24%)
  other arithmetic  56.5 us (19%)
  starting transfers between devices  24.7 us (8%)
  matrix products  20.9 us (7%)
  local copies, waits for them, and re-layouts  20.7 us (7%)
    all_to_all x2, blocking collectives, _exchange(): return lax.all_to_all(x, axis, 0, 0, tiled=False)  92.9 us
    all_to_all x4, waiting for transfers between devices, _exchange(): return lax.all_to_all(x, axis, 0, 0, tiled=False)  71.7 us
    another operation x6, other arithmetic, shards(): lower_factor = jnp.linalg.cholesky(gram_sum)  33.9 us
    all_to_all x4, starting transfers between devices, _exchange(): return lax.all_to_all(x, axis, 0, 0, tiled=False)  24.7 us
    another operation x3, other arithmetic, shards(): inv_lower = jax.scipy.linalg.solve_triangular(lower_factor, eye, lower=True)  19.9 us
    dot_general x9, matrix products, _dot(): return jnp.dot(a, b, precision=lax.Precision.HIGHEST)  19.6 us
  transfers between devices with their start and end apart: 4, of which 3 were waited for; matrix products, arithmetic and copies ran while one was open for 23% of the time, Pallas kernels for 0%

profile of v1, /device:TPU:1, one launch (start us, length us, event | category | flops | bytes accessed | tf_op | source)
XLA Modules:
  0.0 289.9 jit_solution(7130547507691159672)
XLA Ops:
  2.3 24.5 %all_to_all.38 = f32[64,4,256]{2,1,0:T(4,128)S(1)} all-to-all(f32[64,4,256]{2,1,0:T(4,128)S(1)} %reshape.55), channel_id=1, replica_groups=mesh['row'=64,'col'=8] {'row'}, dimensions={0} | all-to-all | bytes 524288 | tf_op jit(solution)/shard_map/all_to_all | solution.py:12
  27.6 4.8 %all-to-all-start.1 = ((f32[64,4,256]{2,1,0:T(4,128)}), f32[64,4,256]{2,1,0:T(4,128)S(1)}, u32[]{:S(2)}, u32[]{:S(2)}) async-start(f32[64,4,256]{2,1,0:T(4,128)} %broadcast_in_dim.14), calls=%async_computation.1 | async-start | bytes 524288 | tf_op jit(solution)/shard_map/all_to_all | solution.py:12
  32.4 13.1 %all-to-all-done.1 = f32[64,4,256]{2,1,0:T(4,128)S(1)} async-done(((f32[64,4,256]{2,1,0:T(4,128)}), f32[64,4,256]{2,1,0:T(4,128)S(1)}, u32[]{:S(2)}, u32[]{:S(2)}) %all-to-all-start.1) | async-done | bytes 262176 | tf_op jit(solution)/shard_map/all_to_all | solution.py:12
  45.4 1.6 broadcast_in_dim.15
  47.0 5.3 %all-to-all-start.2 = ((f32[64,32,256]{2,1,0:T(8,128)}), f32[64,32,256]{2,1,0:T(8,128)S(1)}, u32[]{:S(2)}, u32[]{:S(2)}) async-start(f32[64,32,256]{2,1,0:T(8,128)} %broadcast_in_dim.15), calls=%async_computation.2 | async-start | bytes 4194304 | tf_op jit(solution)/shard_map/all_to_all | solution.py:12
  52.7 11.7 %cholesky.50 = f32[128,128]{1,0:T(8,128)S(1)} custom-call(f32[128,128]{1,0:T(8,128)S(1)} %cholesky.118), custom_call_target="Cholesky" | custom-call | tf_op jit(solution)/shard_map/jit(cholesky)/cholesky | solution.py:29
  64.5 9.8 %custom-call.15 = f32[1,128,128]{1,2,0:T(8,128)S(1)} custom-call(f32[1,128,128]{2,1,0:T(8,128)S(1)} %get-tuple-element.23), custom_call_target="InvertDiagBlocksLowerTriangular" | custom-call | tf_op jit(solution)/shard_map/jit(cholesky)/cholesky | solution.py:29
  74.8 11.7 %cholesky.105 = f32[128,128]{1,0:T(8,128)S(1)} custom-call(f32[128,128]{1,0:T(8,128)S(1)} %convolution_subtract_fusion.3), custom_call_target="Cholesky" | custom-call | tf_op jit(solution)/shard_map/jit(cholesky)/cholesky | solution.py:29
  88.5 3.8 %while.1 = (s32[]{:T(128)}, f32[256,256]{1,0:T(8,128)S(1)}, s32[2,2]{1,0:T(2,128)S(1)}, f32[2,128,128]{2,1,0:T(8,128)S(1)}, s32[]{:T(128)}) while((s32[]{:T(128)}, f32[256,256]{1,0:T(8,128)S(1)}, s32[2,2]{1,0:T(2,128)S(1)}, f32[2,128,128]{2,1,0:T(8,128)S(1)}, s32[]{:T(128)}) %tuple.27), condition=%wide.while_cond, body=%wide.while_body.sunk | while | flops 2 | bytes 131189 | solution.py:31
  92.3 19.8 %custom-call.16 = f32[2,128,128]{1,2,0:T(8,128)S(1)} custom-call(f32[2,128,128]{2,1,0:T(8,128)S(1)} %get-tuple-element.9), custom_call_target="InvertDiagBlocksLowerTriangular" | custom-call | tf_op jit(solution)/shard_map/jit(_solve_triangular)/triangular_solve | solution.py:31
  114.4 3.6 %fusion.3 = f32[2048,256]{1,0:T(8,128)S(1)} fusion(f32[2048,256]{1,0:T(8,128)} %bitcast.58, f32[128,256]{1,0:T(8,128)S(1)} %fusion.8, f32[128,256]{1,0:T(8,128)S(1)} %fusion.5), kind=kOutput, calls=%fused_computation.20 | convolution fusion | flops 1610678272 | bytes 4456448 | tf_op jit(solution)/shard_map/dot_general | solution.py:8
  118.0 3.5 %convolution_bitcast_fusion = f32[256,256]{0,1:T(8,128)S(1)} fusion(f32[2048,256]{1,0:T(8,128)S(1)} %fusion.3, f32[256,2048]{1,0:T(8,128)S(1)} %copy-done.2), kind=kOutput, calls=%fused_computation.10 | convolution fusion | flops 1610612736 | bytes 4456448 | tf_op jit(solution)/shard_map/dot_general | solution.py:8
  123.1 10.0 %all-to-all-start.3 = ((f32[8,256,256]{2,1,0:T(8,128)}), f32[8,256,256]{2,1,0:T(8,128)}, u32[]{:S(2)}, u32[]{:S(2)}) async-start(f32[8,256,256]{2,1,0:T(8,128)} %broadcast_in_dim.16), calls=%async_computation.3 | async-start | bytes 4194304 | tf_op jit(solution)/shard_map/all_to_all | solution.py:12
  133.6 51.3 %all-to-all-done.3 = f32[8,256,256]{2,1,0:T(8,128)} async-done(((f32[8,256,256]{2,1,0:T(8,128)}), f32[8,256,256]{2,1,0:T(8,128)}, u32[]{:S(2)}, u32[]{:S(2)}) %all-to-all-start.3) | async-done | bytes 2097184 | tf_op jit(solution)/shard_map/all_to_all | solution.py:12
  184.9 1.8 reduce_sum.28
  187.4 1.6 all_to_all.28
  189.0 68.4 %all_to_all.39 = f32[64,1,9216]{2,1,0:T(1,128)S(1)} all-to-all(f32[64,1,9216]{2,1,0:T(1,128)S(1)} %all_to_all.28), channel_id=1, replica_groups=mesh['row'=64,'col'=8] {'row'}, dimensions={0} | all-to-all | bytes 4718592 | tf_op jit(solution)/shard_map/all_to_all | solution.py:12
  260.1 4.5 %all-to-all-start.5 = ((f32[64,1,1024]{2,1,0:T(1,128)}), f32[64,1,1024]{2,1,0:T(1,128)S(1)}, u32[]{:S(2)}, u32[]{:S(2)}) async-start(f32[64,1,1024]{2,1,0:T(1,128)} %broadcast_in_dim.19), calls=%async_computation.5 | async-start | bytes 524288 | tf_op jit(solution)/shard_map/all_to_all | solution.py:12
  264.7 3.1 %slice.67 = f32[64,8192]{1,0:T(8,128)} slice(f32[64,9216]{1,0:T(8,128)} %bitcast.57), slice={[0:64], [0:8192]} | slice | bytes 4194304 | tf_op jit(solution)/shard_map/slice | solution.py:49
  267.8 2.7 reshape.59
  270.5 7.3 %all-to-all-done.5 = f32[64,1,1024]{2,1,0:T(1,128)S(1)} async-done(((f32[64,1,1024]{2,1,0:T(1,128)}), f32[64,1,1024]{2,1,0:T(1,128)S(1)}, u32[]{:S(2)}, u32[]{:S(2)}) %all-to-all-start.5) | async-done | bytes 262176 | tf_op jit(solution)/shard_map/all_to_all | solution.py:12
  279.1 3.6 %fusion = f32[2048,256]{1,0:T(8,128)S(1)} fusion(f32[2048,256]{1,0:T(8,128)} %reshape.59, f32[2048,256]{1,0:T(8,128)S(1)} %fusion.3, f32[256,256]{1,0:T(8,128)S(1)} %reshape.60), kind=kOutput, calls=%fused_computation.5 | convolution fusion | flops 1611661312 | bytes 6553600 | tf_op jit(solution)/shard_map/dot_general | solution.py:8
  282.8 3.5 %convolution_subtract_fusion.1 = f32[256,2048]{1,0:T(8,128)S(1)} fusion(f32[256,2048]{1,0:T(8,128)S(1)} %copy-done.3, f32[256,256]{1,0:T(8,128)S(1)} %fusion.4, f32[2048,256]{1,0:T(8,128)S(1)} %fusion), kind=kOutput, calls=%fused_computation.3 | convolution fusion | flops 1611137024 | bytes 6553600 | tf_op jit(solution)/shard_map/dot_general | solution.py:8
  286.3 3.4 %convolution_subtract_fusion = f32[256,2048]{1,0:T(8,128)} fusion(f32[256,2048]{1,0:T(8,128)S(1)} %convolution_subtract_fusion.1, f32[256,256]{1,0:T(8,128)S(1)} %fusion.1, f32[2048,256]{1,0:T(8,128)S(1)} %fusion.3), kind=kOutput, calls=%fused_computation.2 | convolution fusion | flops 1611137024 | bytes 6553600 | tf_op jit(solution)/shard_map/dot_general | solution.py:8
  (57 shorter events, 16.7 us)
Async XLA Ops:
  0.6 1.0 copy-start
  27.6 17.9 %all-to-all-start.1 = ((f32[64,4,256]{2,1,0:T(4,128)}), f32[64,4,256]{2,1,0:T(4,128)S(1)}, u32[]{:S(2)}, u32[]{:S(2)}) async-start(f32[64,4,256]{2,1,0:T(4,128)} %broadcast_in_dim.14), calls=%async_computation.1 | async-start | bytes 524288 | tf_op jit(solution)/shard_map/all_to_all | solution.py:12
  47.0 66.0 %all-to-all-start.2 = ((f32[64,32,256]{2,1,0:T(8,128)}), f32[64,32,256]{2,1,0:T(8,128)S(1)}, u32[]{:S(2)}, u32[]{:S(2)}) async-start(f32[64,32,256]{2,1,0:T(8,128)} %broadcast_in_dim.15), calls=%async_computation.2 | async-start | bytes 4194304 | tf_op jit(solution)/shard_map/all_to_all | solution.py:12
  113.1 1.3 copy-start.4
  114.4 3.6 %copy-start.2 = (f32[256,2048]{1,0:T(8,128)S(1)}, f32[256,2048]{1,0:T(8,128)}, u32[]{:S(2)}) copy-start(f32[256,2048]{1,0:T(8,128)} %param.3) | copy-start | bytes 6291460
  123.1 61.8 %all-to-all-start.3 = ((f32[8,256,256]{2,1,0:T(8,128)}), f32[8,256,256]{2,1,0:T(8,128)}, u32[]{:S(2)}, u32[]{:S(2)}) async-start(f32[8,256,256]{2,1,0:T(8,128)} %broadcast_in_dim.16), calls=%async_computation.3 | async-start | bytes 4194304 | tf_op jit(solution)/shard_map/all_to_all | solution.py:12
  257.9 1.4 copy-start.1
  260.1 17.6 %all-to-all-start.5 = ((f32[64,1,1024]{2,1,0:T(1,128)}), f32[64,1,1024]{2,1,0:T(1,128)S(1)}, u32[]{:S(2)}, u32[]{:S(2)}) async-start(f32[64,1,1024]{2,1,0:T(1,128)} %broadcast_in_dim.19), calls=%async_computation.5 | async-start | bytes 524288 | tf_op jit(solution)/shard_map/all_to_all | solution.py:12
  278.5 4.3 %copy-start.5 = (f32[256,256]{1,0:T(8,128)}, f32[256,256]{1,0:T(8,128)S(1)}, u32[]{:S(2)}) copy-start(f32[256,256]{1,0:T(8,128)S(1)} %reshape.60) | copy-start | bytes 786436
  279.1 3.7 %copy-start.3 = (f32[256,2048]{1,0:T(8,128)S(1)}, f32[256,2048]{1,0:T(8,128)}, u32[]{:S(2)}) copy-start(f32[256,2048]{1,0:T(8,128)} %param.3) | copy-start | bytes 6291460

commit v2 on v1

--- a/solution.py
+++ b/solution.py
@@ -33,11 +33,10 @@
     basis_stored = _dot(panel_stored, inv_lower.T)
 
     partial_sum = _dot(affinity, basis_stored)
-    gathered = _exchange(jnp.broadcast_to(partial_sum[None], (n_col,) + partial_sum.shape), "col")
-    moment_own = gathered.sum(0)
+    own_moment = _exchange(partial_sum.reshape(n_col, piece, k), "col").sum(0)
+    moment_own = _exchange(jnp.broadcast_to(own_moment[None], (n_col, piece, k)), "col").reshape(local_rows, k)
     band_part = _dot(basis_own.T, moment_own)
 
-    own_moment = lax.dynamic_slice_in_dim(moment_own, col_place * piece, piece, 0)
     send = jnp.concatenate(
         [
             jnp.broadcast_to(own_moment.reshape(1, piece * k), (n_row, piece * k)),

time: 294 us -> 260 us (0.88); the launches traced: 290 us -> 260 us
  waiting for transfers between devices: 71.7 us -> 29.3 us
  blocking collectives: 92.9 us -> 117 us
  starting transfers between devices: 24.7 us -> 17.5 us
    all_to_all x4, waiting for transfers between devices: 71.7 us -> 29.3 us  [_exchange(): return lax.all_to_all(x, axis, 0, 0, tiled=False)]
    all_to_all x2 -> x3, blocking collectives: 92.9 us -> 117 us  [_exchange(): return lax.all_to_all(x, axis, 0, 0, tiled=False)]
    all_to_all x4, starting transfers between devices: 24.7 us -> 17.5 us  [_exchange(): return lax.all_to_all(x, axis, 0, 0, tiled=False)]
  transfers between devices with their start and end apart: 4 -> 4, of which waited for: 3 -> 3; matrix products, arithmetic and copies ran while one was open for 23% -> 25% of each run, Pallas kernels for 0% -> 0%
where the time goes in v2:
time: 260 us
  blocking collectives  117 us (45%)
  other arithmetic  54.8 us (21%)
  waiting for transfers between devices  29.3 us (11%)
  local copies, waits for them, and re-layouts  19.8 us (8%)
  matrix products  19.4 us (7%)
  starting transfers between devices  17.5 us (7%)
    all_to_all x3, blocking collectives, _exchange(): return lax.all_to_all(x, axis, 0, 0, tiled=False)  117 us
    another operation x6, other arithmetic, shards(): lower_factor = jnp.linalg.cholesky(gram_sum)  33.9 us
    all_to_all x4, waiting for transfers between devices, _exchange(): return lax.all_to_all(x, axis, 0, 0, tiled=False)  29.3 us
    another operation x3, other arithmetic, shards(): inv_lower = jax.scipy.linalg.solve_triangular(lower_factor, eye, lower=True)  19.9 us
    dot_general x9, matrix products, _dot(): return jnp.dot(a, b, precision=lax.Precision.HIGHEST)  18.1 us
    all_to_all x4, starting transfers between devices, _exchange(): return lax.all_to_all(x, axis, 0, 0, tiled=False)  17.5 us
  transfers between devices with their start and end apart: 4, of which 3 were waited for; matrix products, arithmetic and copies ran while one was open for 25% of the time, Pallas kernels for 0%

profile of v2, /device:TPU:1, one launch (start us, length us, event | category | flops | bytes accessed | tf_op | source)
XLA Modules:
  0.0 259.7 jit_solution(9710865386041563208)
XLA Ops:
  2.3 24.5 %all_to_all.43 = f32[64,4,256]{2,1,0:T(4,128)S(1)} all-to-all(f32[64,4,256]{2,1,0:T(4,128)S(1)} %reshape.61), channel_id=1, replica_groups=mesh['row'=64,'col'=8] {'row'}, dimensions={0} | all-to-all | bytes 524288 | tf_op jit(solution)/shard_map/all_to_all | solution.py:12
  27.6 4.8 %all-to-all-start.1 = ((f32[64,4,256]{2,1,0:T(4,128)}), f32[64,4,256]{2,1,0:T(4,128)S(1)}, u32[]{:S(2)}, u32[]{:S(2)}) async-start(f32[64,4,256]{2,1,0:T(4,128)} %broadcast_in_dim.14), calls=%async_computation.1 | async-start | bytes 524288 | tf_op jit(solution)/shard_map/all_to_all | solution.py:12
  32.4 13.1 %all-to-all-done.1 = f32[64,4,256]{2,1,0:T(4,128)S(1)} async-done(((f32[64,4,256]{2,1,0:T(4,128)}), f32[64,4,256]{2,1,0:T(4,128)S(1)}, u32[]{:S(2)}, u32[]{:S(2)}) %all-to-all-start.1) | async-done | bytes 262176 | tf_op jit(solution)/shard_map/all_to_all | solution.py:12
  45.4 1.6 broadcast_in_dim.15
  47.0 4.8 %all-to-all-start.2 = ((f32[64,32,256]{2,1,0:T(8,128)}), f32[64,32,256]{2,1,0:T(8,128)S(1)}, u32[]{:S(2)}, u32[]{:S(2)}) async-start(f32[64,32,256]{2,1,0:T(8,128)} %broadcast_in_dim.15), calls=%async_computation.2 | async-start | bytes 4194304 | tf_op jit(solution)/shard_map/all_to_all | solution.py:12
  52.1 11.7 %cholesky.50 = f32[128,128]{1,0:T(8,128)S(1)} custom-call(f32[128,128]{1,0:T(8,128)S(1)} %cholesky.118), custom_call_target="Cholesky" | custom-call | tf_op jit(solution)/shard_map/jit(cholesky)/cholesky | solution.py:29
  63.9 9.8 %custom-call.15 = f32[1,128,128]{1,2,0:T(8,128)S(1)} custom-call(f32[1,128,128]{2,1,0:T(8,128)S(1)} %get-tuple-element.23), custom_call_target="InvertDiagBlocksLowerTriangular" | custom-call | tf_op jit(solution)/shard_map/jit(cholesky)/cholesky | solution.py:29
  74.2 11.7 %cholesky.105 = f32[128,128]{1,0:T(8,128)S(1)} custom-call(f32[128,128]{1,0:T(8,128)S(1)} %convolution_subtract_fusion.3), custom_call_target="Cholesky" | custom-call | tf_op jit(solution)/shard_map/jit(cholesky)/cholesky | solution.py:29
  87.9 3.8 %while.1 = (s32[]{:T(128)}, f32[256,256]{1,0:T(8,128)S(1)}, s32[2,2]{1,0:T(2,128)S(1)}, f32[2,128,128]{2,1,0:T(8,128)S(1)}, s32[]{:T(128)}) while((s32[]{:T(128)}, f32[256,256]{1,0:T(8,128)S(1)}, s32[2,2]{1,0:T(2,128)S(1)}, f32[2,128,128]{2,1,0:T(8,128)S(1)}, s32[]{:T(128)}) %tuple.27), condition=%wide.while_cond, body=%wide.while_body.sunk | while | flops 2 | bytes 131189 | solution.py:31
  91.8 19.9 %custom-call.16 = f32[2,128,128]{1,2,0:T(8,128)S(1)} custom-call(f32[2,128,128]{2,1,0:T(8,128)S(1)} %get-tuple-element.9), custom_call_target="InvertDiagBlocksLowerTriangular" | custom-call | tf_op jit(solution)/shard_map/jit(_solve_triangular)/triangular_solve | solution.py:31
  113.8 3.6 %fusion.3 = f32[2048,256]{1,0:T(8,128)S(1)} fusion(f32[2048,256]{1,0:T(8,128)} %bitcast.59, f32[128,256]{1,0:T(8,128)S(1)} %fusion.8, f32[128,256]{1,0:T(8,128)S(1)} %fusion.5), kind=kOutput, calls=%fused_computation.19 | convolution fusion | flops 1610678272 | bytes 4456448 | tf_op jit(solution)/shard_map/dot_general | solution.py:8
  117.4 2.0 fusion.16
  119.5 20.4 %all_to_all.44 = f32[8,32,256]{2,1,0:T(8,128)S(1)} all-to-all(f32[8,32,256]{2,1,0:T(8,128)S(1)} %bitcast.62), channel_id=1, replica_groups=mesh['row'=64,'col'=8] {'col'}, dimensions={0} | all-to-all | bytes 524288 | tf_op jit(solution)/shard_map/all_to_all | solution.py:12
  140.6 3.4 %all-to-all-start.4 = ((f32[8,32,256]{2,1,0:T(8,128)}), f32[8,32,256]{2,1,0:T(8,128)S(1)}, u32[]{:S(2)}, u32[]{:S(2)}) async-start(f32[8,32,256]{2,1,0:T(8,128)} %broadcast_in_dim.18), calls=%async_computation.4 | async-start | bytes 524288 | tf_op jit(solution)/shard_map/all_to_all | solution.py:12
  144.5 9.0 %all-to-all-done.4 = f32[8,32,256]{2,1,0:T(8,128)S(1)} async-done(((f32[8,32,256]{2,1,0:T(8,128)}), f32[8,32,256]{2,1,0:T(8,128)S(1)}, u32[]{:S(2)}, u32[]{:S(2)}) %all-to-all-start.4) | async-done | bytes 262176 | tf_op jit(solution)/shard_map/all_to_all | solution.py:12
  154.1 1.6 all_to_all.32
  155.7 71.8 %all_to_all.45 = f32[64,1,9216]{2,1,0:T(1,128)S(1)} all-to-all(f32[64,1,9216]{2,1,0:T(1,128)S(1)} %all_to_all.32), channel_id=1, replica_groups=mesh['row'=64,'col'=8] {'row'}, dimensions={0} | all-to-all | bytes 4718592 | tf_op jit(solution)/shard_map/all_to_all | solution.py:12
  230.2 4.5 %all-to-all-start.6 = ((f32[64,1,1024]{2,1,0:T(1,128)}), f32[64,1,1024]{2,1,0:T(1,128)S(1)}, u32[]{:S(2)}, u32[]{:S(2)}) async-start(f32[64,1,1024]{2,1,0:T(1,128)} %broadcast_in_dim.19), calls=%async_computation.6 | async-start | bytes 524288 | tf_op jit(solution)/shard_map/all_to_all | solution.py:12
  234.7 3.1 %slice.67 = f32[64,8192]{1,0:T(8,128)} slice(f32[64,9216]{1,0:T(8,128)} %bitcast.58), slice={[0:64], [0:8192]} | slice | bytes 4194304 | tf_op jit(solution)/shard_map/slice | solution.py:48
  237.8 2.7 %reshape.67 = f32[2048,256]{1,0:T(8,128)} reshape(f32[64,8192]{1,0:T(8,128)} %slice.67) | data formatting | bytes 4194304 | tf_op jit(solution)/shard_map/reshape | solution.py:48
  240.5 7.3 %all-to-all-done.6 = f32[64,1,1024]{2,1,0:T(1,128)S(1)} async-done(((f32[64,1,1024]{2,1,0:T(1,128)}), f32[64,1,1024]{2,1,0:T(1,128)S(1)}, u32[]{:S(2)}, u32[]{:S(2)}) %all-to-all-start.6) | async-done | bytes 262176 | tf_op jit(solution)/shard_map/all_to_all | solution.py:12
  249.2 3.6 %fusion = f32[2048,256]{1,0:T(8,128)S(1)} fusion(f32[2048,256]{1,0:T(8,128)} %reshape.67, f32[2048,256]{1,0:T(8,128)S(1)} %fusion.3, f32[256,256]{1,0:T(8,128)S(1)} %reshape.68), kind=kOutput, calls=%fused_computation.5 | convolution fusion | flops 1611661312 | bytes 6553600 | tf_op jit(solution)/shard_map/dot_general | solution.py:8
  252.8 3.5 %convolution_subtract_fusion.1 = f32[256,2048]{1,0:T(8,128)S(1)} fusion(f32[256,2048]{1,0:T(8,128)S(1)} %copy-done.3, f32[256,256]{1,0:T(8,128)S(1)} %fusion.4, f32[2048,256]{1,0:T(8,128)S(1)} %fusion), kind=kOutput, calls=%fused_computation.3 | convolution fusion | flops 1611137024 | bytes 6553600 | tf_op jit(solution)/shard_map/dot_general | solution.py:8
  256.4 3.3 %convolution_subtract_fusion = f32[256,2048]{1,0:T(8,128)} fusion(f32[256,2048]{1,0:T(8,128)S(1)} %convolution_subtract_fusion.1, f32[256,256]{1,0:T(8,128)S(1)} %fusion.1, f32[2048,256]{1,0:T(8,128)S(1)} %fusion.3), kind=kOutput, calls=%fused_computation.2 | convolution fusion | flops 1611137024 | bytes 6553600 | tf_op jit(solution)/shard_map/dot_general | solution.py:8
  (56 shorter events, 15.8 us)
Async XLA Ops:
  0.6 1.0 copy-start
  27.6 17.9 %all-to-all-start.1 = ((f32[64,4,256]{2,1,0:T(4,128)}), f32[64,4,256]{2,1,0:T(4,128)S(1)}, u32[]{:S(2)}, u32[]{:S(2)}) async-start(f32[64,4,256]{2,1,0:T(4,128)} %broadcast_in_dim.14), calls=%async_computation.1 | async-start | bytes 524288 | tf_op jit(solution)/shard_map/all_to_all | solution.py:12
  47.0 65.5 %all-to-all-start.2 = ((f32[64,32,256]{2,1,0:T(8,128)}), f32[64,32,256]{2,1,0:T(8,128)S(1)}, u32[]{:S(2)}, u32[]{:S(2)}) async-start(f32[64,32,256]{2,1,0:T(8,128)} %broadcast_in_dim.15), calls=%async_computation.2 | async-start | bytes 4194304 | tf_op jit(solution)/shard_map/all_to_all | solution.py:12
  112.5 1.3 copy-start.4
  113.8 3.6 %copy-start.2 = (f32[256,2048]{1,0:T(8,128)S(1)}, f32[256,2048]{1,0:T(8,128)}, u32[]{:S(2)}) copy-start(f32[256,2048]{1,0:T(8,128)} %param.3) | copy-start | bytes 6291460
  140.6 12.8 %all-to-all-start.4 = ((f32[8,32,256]{2,1,0:T(8,128)}), f32[8,32,256]{2,1,0:T(8,128)S(1)}, u32[]{:S(2)}, u32[]{:S(2)}) async-start(f32[8,32,256]{2,1,0:T(8,128)} %broadcast_in_dim.18), calls=%async_computation.4 | async-start | bytes 524288 | tf_op jit(solution)/shard_map/all_to_all | solution.py:12
  227.9 1.4 copy-start.1
  230.2 17.7 %all-to-all-start.6 = ((f32[64,1,1024]{2,1,0:T(1,128)}), f32[64,1,1024]{2,1,0:T(1,128)S(1)}, u32[]{:S(2)}, u32[]{:S(2)}) async-start(f32[64,1,1024]{2,1,0:T(1,128)} %broadcast_in_dim.19), calls=%async_computation.6 | async-start | bytes 524288 | tf_op jit(solution)/shard_map/all_to_all | solution.py:12
  248.5 4.3 %copy-start.5 = (f32[256,256]{1,0:T(8,128)}, f32[256,256]{1,0:T(8,128)S(1)}, u32[]{:S(2)}) copy-start(f32[256,256]{1,0:T(8,128)S(1)} %reshape.68) | copy-start | bytes 786436
  249.2 3.7 %copy-start.3 = (f32[256,2048]{1,0:T(8,128)S(1)}, f32[256,2048]{1,0:T(8,128)}, u32[]{:S(2)}) copy-start(f32[256,2048]{1,0:T(8,128)} %param.3) | copy-start | bytes 6291460

commit v3 on v2

--- a/solution.py
+++ b/solution.py
@@ -10,6 +10,19 @@
 
 def _exchange(x, axis):
     return lax.all_to_all(x, axis, 0, 0, tiled=False)
+
+
+def _inverse_cholesky(gram):
+    h = gram.shape[0] // 2
+    eye = jnp.eye(h, dtype=gram.dtype)
+    l11 = jnp.linalg.cholesky(gram[:h, :h])
+    i11 = jax.scipy.linalg.solve_triangular(l11, eye, lower=True)
+    l21 = _dot(gram[h:, :h], i11.T)
+    l22 = jnp.linalg.cholesky(gram[h:, h:] - _dot(l21, l21.T))
+    i22 = jax.scipy.linalg.solve_triangular(l22, eye, lower=True)
+    i21 = -_dot(i22, _dot(l21, i11))
+    top = jnp.concatenate([i11, jnp.zeros_like(i11)], axis=1)
+    return jnp.concatenate([top, jnp.concatenate([i21, i22], axis=1)], axis=0)
 
 
 def shards(panel_cols, affinity):
@@ -26,9 +39,7 @@
     own_panel = lax.dynamic_slice_in_dim(panel_cols, col_place * piece, piece, 0)
     panel_stored = _exchange(jnp.broadcast_to(own_panel[None], (n_row, piece, k)), "row").reshape(n_row * piece, k)
 
-    lower_factor = jnp.linalg.cholesky(gram_sum)
-    eye = jnp.eye(k, dtype=panel_cols.dtype)
-    inv_lower = jax.scipy.linalg.solve_triangular(lower_factor, eye, lower=True)
+    inv_lower = _inverse_cholesky(gram_sum)
     basis_own = _dot(panel_cols, inv_lower.T)
     basis_stored = _dot(panel_stored, inv_lower.T)
 

time: 260 us -> 248 us (0.954)
  other arithmetic: 54.8 us -> 46.8 us
  local copies, waits for them, and re-layouts: 19.8 us -> 16.1 us
    another operation x9 -> x10, other arithmetic: 53.9 us -> 45.9 us  [the longest x3 12.4 us: _inverse_cholesky(): l11 = jnp.linalg.cholesky(gram[:h, :h])]
    another operation x9 -> x1, local copies, waits for them, and re-layouts: 3.88 us -> 0.09 us  [_inverse_cholesky(): i22 = jax.scipy.linalg.solve_triangular(l22, eye, lower=True)]
    dot_general x9 -> x13, matrix products: 18.1 us -> 19.1 us  [_dot(): return jnp.dot(a, b, precision=lax.Precision.HIGHEST)]
  transfers between devices with their start and end apart: 4 -> 4, of which waited for: 3 -> 4; matrix products, arithmetic and copies ran while one was open for 25% -> 22% of each run, Pallas kernels for 0% -> 0%
where the time goes in v3:
time: 248 us; the launch traced here: 247 us
  blocking collectives  115 us (46%)
  other arithmetic  46.8 us (19%)
  waiting for transfers between devices  30.7 us (12%)
  matrix products  19.7 us (8%)
  starting transfers between devices  17.7 us (7%)
  local copies, waits for them, and re-layouts  16.1 us (6%)
    all_to_all x3, blocking collectives, _exchange(): return lax.all_to_all(x, axis, 0, 0, tiled=False)  115 us
    all_to_all x4, waiting for transfers between devices, _exchange(): return lax.all_to_all(x, axis, 0, 0, tiled=False)  30.7 us
    dot_general x13, matrix products, _dot(): return jnp.dot(a, b, precision=lax.Precision.HIGHEST)  19.1 us
    all_to_all x4, starting transfers between devices, _exchange(): return lax.all_to_all(x, axis, 0, 0, tiled=False)  17.7 us
    another operation x3, other arithmetic, _inverse_cholesky(): l11 = jnp.linalg.cholesky(gram[:h, :h])  12.4 us
    another operation x3, other arithmetic, _inverse_cholesky(): l22 = jnp.linalg.cholesky(gram[h:, h:] - _dot(l21, l21.T))  12.4 us
    another operation x2, other arithmetic, _inverse_cholesky(): i22 = jax.scipy.linalg.solve_triangular(l22, eye, lower=True)  10.6 us
    another operation x2, other arithmetic, _inverse_cholesky(): i11 = jax.scipy.linalg.solve_triangular(l11, eye, lower=True)  10.5 us
  transfers between devices with their start and end apart: 4, of which 4 were waited for; matrix products, arithmetic and copies ran while one was open for 22% of the time, Pallas kernels for 0%

profile of v3, /device:TPU:1, one launch (start us, length us, event | category | flops | bytes accessed | tf_op | source)
XLA Modules:
  0.0 247.2 jit_solution(3393981573886944447)
XLA Ops:
  2.3 24.5 %all_to_all.43 = f32[64,4,256]{2,1,0:T(4,128)S(1)} all-to-all(f32[64,4,256]{2,1,0:T(4,128)S(1)} %reshape.50), channel_id=1, replica_groups=mesh['row'=64,'col'=8] {'row'}, dimensions={0} | all-to-all | bytes 524288 | tf_op jit(solution)/shard_map/all_to_all | solution.py:12
  27.6 4.8 %all-to-all-start.1 = ((f32[64,4,256]{2,1,0:T(4,128)}), f32[64,4,256]{2,1,0:T(4,128)S(1)}, u32[]{:S(2)}, u32[]{:S(2)}) async-start(f32[64,4,256]{2,1,0:T(4,128)} %broadcast_in_dim.13), calls=%async_computation.1 | async-start | bytes 524288 | tf_op jit(solution)/shard_map/all_to_all | solution.py:12
  32.4 13.1 %all-to-all-done.1 = f32[64,4,256]{2,1,0:T(4,128)S(1)} async-done(((f32[64,4,256]{2,1,0:T(4,128)}), f32[64,4,256]{2,1,0:T(4,128)S(1)}, u32[]{:S(2)}, u32[]{:S(2)}) %all-to-all-start.1) | async-done | bytes 262176 | tf_op jit(solution)/shard_map/all_to_all | solution.py:12
  45.4 1.6 broadcast_in_dim.14
  47.0 5.0 %all-to-all-start.2 = ((f32[64,32,256]{2,1,0:T(8,128)}), f32[64,32,256]{2,1,0:T(8,128)S(1)}, u32[]{:S(2)}, u32[]{:S(2)}) async-start(f32[64,32,256]{2,1,0:T(8,128)} %broadcast_in_dim.14), calls=%async_computation.2 | async-start | bytes 4194304 | tf_op jit(solution)/shard_map/all_to_all | solution.py:12
  52.3 11.7 %cholesky.44 = f32[128,128]{1,0:T(8,128)S(1)} custom-call(f32[128,128]{1,0:T(8,128)S(1)} %get-tuple-element.5), custom_call_target="Cholesky" | custom-call | tf_op jit(solution)/shard_map/jit(cholesky)/cholesky | solution.py:18
  65.4 9.8 %custom-call.6 = f32[1,128,128]{1,2,0:T(8,128)S(1)} custom-call(f32[1,128,128]{2,1,0:T(8,128)S(1)} %fusion.12), custom_call_target="InvertDiagBlocksLowerTriangular" | custom-call | tf_op jit(solution)/shard_map/jit(_solve_triangular)/triangular_solve | solution.py:19
  76.1 11.7 %cholesky.55 = f32[128,128]{1,0:T(8,128)S(1)} custom-call(f32[128,128]{1,0:T(8,128)S(1)} %fusion.17), custom_call_target="Cholesky" | custom-call | tf_op jit(solution)/shard_map/jit(cholesky)/cholesky | solution.py:21
  89.2 10.0 %custom-call.7 = f32[1,128,128]{1,2,0:T(8,128)S(1)} custom-call(f32[1,128,128]{2,1,0:T(8,128)S(1)} %fusion.13), custom_call_target="InvertDiagBlocksLowerTriangular" | custom-call | tf_op jit(solution)/shard_map/jit(_solve_triangular)/triangular_solve | solution.py:22
  100.1 1.4 all-to-all-done.2
  102.8 3.6 %fusion.2 = f32[2048,256]{1,0:T(8,128)S(1)} fusion(f32[2048,256]{1,0:T(8,128)} %bitcast.53, f32[128,128]{1,0:T(8,128)S(1)} %fusion.10, f32[128,128]{1,0:T(8,128)S(1)} %copy.22, f32[128,128]{1,0:T(8,128)S(1)} %convolution_negate_fusion), kind=kOutput, calls=%fused_computation.13 | convolution fusion | flops 1610874880 | bytes 4390912 | tf_op jit(solution)/shard_map/dot_general | solution.py:8
  106.4 2.0 fusion.29
  108.4 19.3 %all_to_all.44 = f32[8,32,256]{2,1,0:T(8,128)S(1)} all-to-all(f32[8,32,256]{2,1,0:T(8,128)S(1)} %bitcast.56), channel_id=1, replica_groups=mesh['row'=64,'col'=8] {'col'}, dimensions={0} | all-to-all | bytes 524288 | tf_op jit(solution)/shard_map/all_to_all | solution.py:12
  128.4 3.4 %all-to-all-start.4 = ((f32[8,32,256]{2,1,0:T(8,128)}), f32[8,32,256]{2,1,0:T(8,128)S(1)}, u32[]{:S(2)}, u32[]{:S(2)}) async-start(f32[8,32,256]{2,1,0:T(8,128)} %broadcast_in_dim.17), calls=%async_computation.4 | async-start | bytes 524288 | tf_op jit(solution)/shard_map/all_to_all | solution.py:12
  132.3 8.9 %all-to-all-done.4 = f32[8,32,256]{2,1,0:T(8,128)S(1)} async-done(((f32[8,32,256]{2,1,0:T(8,128)}), f32[8,32,256]{2,1,0:T(8,128)S(1)}, u32[]{:S(2)}, u32[]{:S(2)}) %all-to-all-start.4) | async-done | bytes 262176 | tf_op jit(solution)/shard_map/all_to_all | solution.py:12
  141.8 1.6 all_to_all.32
  143.5 71.5 %all_to_all.45 = f32[64,1,9216]{2,1,0:T(1,128)S(1)} all-to-all(f32[64,1,9216]{2,1,0:T(1,128)S(1)} %all_to_all.32), channel_id=1, replica_groups=mesh['row'=64,'col'=8] {'row'}, dimensions={0} | all-to-all | bytes 4718592 | tf_op jit(solution)/shard_map/all_to_all | solution.py:12
  217.7 4.6 %all-to-all-start.6 = ((f32[64,1,1024]{2,1,0:T(1,128)}), f32[64,1,1024]{2,1,0:T(1,128)S(1)}, u32[]{:S(2)}, u32[]{:S(2)}) async-start(f32[64,1,1024]{2,1,0:T(1,128)} %broadcast_in_dim.18), calls=%async_computation.6 | async-start | bytes 524288 | tf_op jit(solution)/shard_map/all_to_all | solution.py:12
  222.3 3.1 %slice.31 = f32[64,8192]{1,0:T(8,128)} slice(f32[64,9216]{1,0:T(8,128)} %bitcast.52), slice={[0:64], [0:8192]} | slice | bytes 4194304 | tf_op jit(solution)/shard_map/slice | solution.py:59
  225.3 2.7 %reshape.56 = f32[2048,256]{1,0:T(8,128)} reshape(f32[64,8192]{1,0:T(8,128)} %slice.31) | data formatting | bytes 4194304 | tf_op jit(solution)/shard_map/reshape | solution.py:59
  228.1 7.3 %all-to-all-done.6 = f32[64,1,1024]{2,1,0:T(1,128)S(1)} async-done(((f32[64,1,1024]{2,1,0:T(1,128)}), f32[64,1,1024]{2,1,0:T(1,128)S(1)}, u32[]{:S(2)}, u32[]{:S(2)}) %all-to-all-start.6) | async-done | bytes 262176 | tf_op jit(solution)/shard_map/all_to_all | solution.py:12
  236.7 3.6 %fusion = f32[2048,256]{1,0:T(8,128)S(1)} fusion(f32[2048,256]{1,0:T(8,128)} %reshape.56, f32[2048,256]{1,0:T(8,128)S(1)} %fusion.2, f32[256,256]{1,0:T(8,128)S(1)} %reshape.57), kind=kOutput, calls=%fused_computation.3 | convolution fusion | flops 1611661312 | bytes 6553600 | tf_op jit(solution)/shard_map/dot_general | solution.py:8
  240.3 3.5 %convolution_subtract_fusion.1 = f32[256,2048]{1,0:T(8,128)S(1)} fusion(f32[256,2048]{1,0:T(8,128)S(1)} %copy-done.3, f32[256,256]{1,0:T(8,128)S(1)} %fusion.3, f32[2048,256]{1,0:T(8,128)S(1)} %fusion), kind=kOutput, calls=%fused_computation.1 | convolution fusion | flops 1611137024 | bytes 6553600 | tf_op jit(solution)/shard_map/dot_general | solution.py:8
  243.9 3.3 %convolution_subtract_fusion = f32[256,2048]{1,0:T(8,128)} fusion(f32[256,2048]{1,0:T(8,128)S(1)} %convolution_subtract_fusion.1, f32[256,256]{1,0:T(8,128)S(1)} %fusion.1, f32[2048,256]{1,0:T(8,128)S(1)} %fusion.2), kind=kOutput, calls=%fused_computation | convolution fusion | flops 1611137024 | bytes 6553600 | tf_op jit(solution)/shard_map/dot_general | solution.py:8
  (51 shorter events, 14.3 us)
Async XLA Ops:
  0.6 1.0 copy-start
  27.6 17.9 %all-to-all-start.1 = ((f32[64,4,256]{2,1,0:T(4,128)}), f32[64,4,256]{2,1,0:T(4,128)S(1)}, u32[]{:S(2)}, u32[]{:S(2)}) async-start(f32[64,4,256]{2,1,0:T(4,128)} %broadcast_in_dim.13), calls=%async_computation.1 | async-start | bytes 524288 | tf_op jit(solution)/shard_map/all_to_all | solution.py:12
  47.0 54.5 %all-to-all-start.2 = ((f32[64,32,256]{2,1,0:T(8,128)}), f32[64,32,256]{2,1,0:T(8,128)S(1)}, u32[]{:S(2)}, u32[]{:S(2)}) async-start(f32[64,32,256]{2,1,0:T(8,128)} %broadcast_in_dim.14), calls=%async_computation.2 | async-start | bytes 4194304 | tf_op jit(solution)/shard_map/all_to_all | solution.py:12
  101.5 1.3 copy-start.4
  102.8 3.6 %copy-start.2 = (f32[256,2048]{1,0:T(8,128)S(1)}, f32[256,2048]{1,0:T(8,128)}, u32[]{:S(2)}) copy-start(f32[256,2048]{1,0:T(8,128)} %param.6) | copy-start | bytes 6291460
  128.4 12.8 %all-to-all-start.4 = ((f32[8,32,256]{2,1,0:T(8,128)}), f32[8,32,256]{2,1,0:T(8,128)S(1)}, u32[]{:S(2)}, u32[]{:S(2)}) async-start(f32[8,32,256]{2,1,0:T(8,128)} %broadcast_in_dim.17), calls=%async_computation.4 | async-start | bytes 524288 | tf_op jit(solution)/shard_map/all_to_all | solution.py:12
  215.4 1.4 copy-start.1
  217.7 17.6 %all-to-all-start.6 = ((f32[64,1,1024]{2,1,0:T(1,128)}), f32[64,1,1024]{2,1,0:T(1,128)S(1)}, u32[]{:S(2)}, u32[]{:S(2)}) async-start(f32[64,1,1024]{2,1,0:T(1,128)} %broadcast_in_dim.18), calls=%async_computation.6 | async-start | bytes 524288 | tf_op jit(solution)/shard_map/all_to_all | solution.py:12
  236.0 4.3 %copy-start.5 = (f32[256,256]{1,0:T(8,128)}, f32[256,256]{1,0:T(8,128)S(1)}, u32[]{:S(2)}) copy-start(f32[256,256]{1,0:T(8,128)S(1)} %reshape.57) | copy-start | bytes 786436
  236.7 3.7 %copy-start.3 = (f32[256,2048]{1,0:T(8,128)S(1)}, f32[256,2048]{1,0:T(8,128)}, u32[]{:S(2)}) copy-start(f32[256,2048]{1,0:T(8,128)} %param.6) | copy-start | bytes 6291460

commit v4 on v2

--- a/solution.py
+++ b/solution.py
@@ -1,6 +1,8 @@
 import jax
 import jax.numpy as jnp
 from jax import lax
+from jax.experimental import pallas as pl
+from jax.experimental.pallas import tpu as pltpu
 from jax.sharding import PartitionSpec as P
 
 
@@ -10,6 +12,57 @@
 
 def _exchange(x, axis):
     return lax.all_to_all(x, axis, 0, 0, tiled=False)
+
+
+def _inverse_cholesky_kernel(g_ref, w_ref, a_ref):
+    n = g_ref.shape[0]
+    h = n // 2
+    rows = lax.broadcasted_iota(jnp.int32, (n, n), 0)
+    cols = lax.broadcasted_iota(jnp.int32, (n, n), 1)
+    a_ref[...] = g_ref[...]
+    w_ref[...] = jnp.where(rows == cols, 1.0, 0.0).astype(w_ref.dtype)
+    lane = lax.broadcasted_iota(jnp.int32, (1, n), 1)
+
+    sub = lax.broadcasted_iota(jnp.int32, (8, n), 0)
+
+    def row_of(ref, k, width):
+        base = pl.multiple_of((k // 8) * 8, 8)
+        block = ref[pl.ds(base, 8), :width]
+        return jnp.sum(jnp.where(sub[:, :width] == k - base, block, 0.0), axis=0, keepdims=True)
+
+    def step(k, lo, w_cols):
+        row_a = row_of(a_ref, k, n)
+        piv = jnp.sum(jnp.where(lane == k, row_a, 0.0))
+        col = jnp.broadcast_to(row_a, (8, n)).T[lo:, 0:1]
+        ridx = lax.broadcasted_iota(jnp.int32, (n - lo, 1), 0) + lo
+        f = jnp.where(ridx > k, col / piv, 0.0)
+        a_ref[lo:, lo:] = a_ref[lo:, lo:] - f * row_a[:, lo:]
+        w_ref[lo:, :w_cols] = w_ref[lo:, :w_cols] - f * row_of(w_ref, k, w_cols)
+
+    def first(k, c):
+        step(k, 0, h)
+        return c
+
+    def second(k, c):
+        step(k, h, n)
+        return c
+
+    lax.fori_loop(0, h, first, 0)
+    lax.fori_loop(h, n, second, 0)
+    diag = jnp.sum(jnp.where(rows == cols, a_ref[...], 0.0), axis=1, keepdims=True)
+    w_ref[...] = w_ref[...] / jnp.sqrt(diag)
+
+
+def _inverse_cholesky(gram):
+    n = gram.shape[0]
+    return pl.pallas_call(
+        _inverse_cholesky_kernel,
+        out_shape=jax.ShapeDtypeStruct((n, n), gram.dtype),
+        in_specs=[pl.BlockSpec(memory_space=pltpu.VMEM)],
+        out_specs=pl.BlockSpec(memory_space=pltpu.VMEM),
+        scratch_shapes=[pltpu.VMEM((n, n), gram.dtype)],
+        cost_estimate=pl.CostEstimate(flops=2 * n * n * n, bytes_accessed=8 * n * n, transcendentals=n),
+    )(gram)
 
 
 def shards(panel_cols, affinity):
@@ -26,9 +79,7 @@
     own_panel = lax.dynamic_slice_in_dim(panel_cols, col_place * piece, piece, 0)
     panel_stored = _exchange(jnp.broadcast_to(own_panel[None], (n_row, piece, k)), "row").reshape(n_row * piece, k)
 
-    lower_factor = jnp.linalg.cholesky(gram_sum)
-    eye = jnp.eye(k, dtype=panel_cols.dtype)
-    inv_lower = jax.scipy.linalg.solve_triangular(lower_factor, eye, lower=True)
+    inv_lower = _inverse_cholesky(gram_sum)
     basis_own = _dot(panel_cols, inv_lower.T)
     basis_stored = _dot(panel_stored, inv_lower.T)
 

time: 260 us -> 270 us (1.038)
  Pallas kernels: 0 us -> 69.6 us
  other arithmetic: 54.8 us -> 0.9 us
  local copies, waits for them, and re-layouts: 19.8 us -> 16.4 us
    pallas_call x0 -> x1, Pallas kernels: none -> 69.6 us  [_inverse_cholesky(): pl.pallas_call(_inverse_cholesky_kernel, out_shape=jax.ShapeDtypeStruct((...]
    another operation x9 -> x0, other arithmetic: 53.9 us -> none  [the longest x6 33.9 us: shards(): lower_factor = jnp.linalg.cholesky(gram_sum)]
    another operation x9 -> x0, local copies, waits for them, and re-layouts: 3.88 us -> none
  transfers between devices with their start and end apart: 4 -> 4, of which waited for: 3 -> 3; matrix products, arithmetic and copies ran while one was open for 25% -> 3% of each run, Pallas kernels for 0% -> 26%
where the time goes in v4:
time: 270 us; the launch traced here: 269 us
  blocking collectives  117 us (43%)
  Pallas kernels  69.6 us (26%)
  waiting for transfers between devices  29 us (11%)
  matrix products  18.1 us (7%)
  starting transfers between devices  17.5 us (6%)
  local copies, waits for them, and re-layouts  16.4 us (6%)
    all_to_all x3, blocking collectives, _exchange(): return lax.all_to_all(x, axis, 0, 0, tiled=False)  117 us
    pallas_call x1, Pallas kernels, _inverse_cholesky(): pl.pallas_call(_inverse_cholesky_kernel, out_shape=jax.ShapeDtypeStruct((...  69.6 us
    all_to_all x4, waiting for transfers between devices, _exchange(): return lax.all_to_all(x, axis, 0, 0, tiled=False)  29 us
    dot_general x9, matrix products, _dot(): return jnp.dot(a, b, precision=lax.Precision.HIGHEST)  18.1 us
    all_to_all x4, starting transfers between devices, _exchange(): return lax.all_to_all(x, axis, 0, 0, tiled=False)  17.5 us
  transfers between devices with their start and end apart: 4, of which 3 were waited for; matrix products, arithmetic and copies ran while one was open for 3% of the time, Pallas kernels for 26%

profile of v4, /device:TPU:1, one launch (start us, length us, event | category | flops | bytes accessed | tf_op | source)
XLA Modules:
  0.0 269.4 jit_solution(14778419289330287288)
XLA Ops:
  0.6 0.9 copy-done
  2.3 24.5 %all_to_all.43 = f32[64,4,256]{2,1,0:T(4,128)S(1)} all-to-all(f32[64,4,256]{2,1,0:T(4,128)S(1)} %reshape.42), channel_id=1, replica_groups=mesh['row'=64,'col'=8] {'row'}, dimensions={0} | all-to-all | bytes 524288 | tf_op jit(solution)/shard_map/all_to_all | solution.py:14
  27.6 4.8 %all-to-all-start.1 = ((f32[64,4,256]{2,1,0:T(4,128)}), f32[64,4,256]{2,1,0:T(4,128)S(1)}, u32[]{:S(2)}, u32[]{:S(2)}) async-start(f32[64,4,256]{2,1,0:T(4,128)} %broadcast_in_dim.12), calls=%async_computation.1 | async-start | bytes 524288 | tf_op jit(solution)/shard_map/all_to_all | solution.py:14
  32.4 13.1 %all-to-all-done.1 = f32[64,4,256]{2,1,0:T(4,128)S(1)} async-done(((f32[64,4,256]{2,1,0:T(4,128)}), f32[64,4,256]{2,1,0:T(4,128)S(1)}, u32[]{:S(2)}, u32[]{:S(2)}) %all-to-all-start.1) | async-done | bytes 262176 | tf_op jit(solution)/shard_map/all_to_all | solution.py:14
  45.4 1.6 broadcast_in_dim.13
  47.0 4.8 %all-to-all-start.2 = ((f32[64,32,256]{2,1,0:T(8,128)}), f32[64,32,256]{2,1,0:T(8,128)S(1)}, u32[]{:S(2)}, u32[]{:S(2)}) async-start(f32[64,32,256]{2,1,0:T(8,128)} %broadcast_in_dim.13), calls=%async_computation.2 | async-start | bytes 4194304 | tf_op jit(solution)/shard_map/all_to_all | solution.py:14
  52.6 69.6 %shard_map.41 = f32[256,256]{1,0:T(8,128)} custom-call(f32[256,256]{1,0:T(8,128)} %reshape.43.g_ref), custom_call_target="tpu_custom_call" | custom-call | flops 33554432 | bytes 524288 | tf_op jit(solution)/shard_map/pallas_call | solution.py:58
  122.2 1.3 copy-done.4
  123.6 3.6 %fusion.4 = f32[2048,256]{1,0:T(8,128)S(1)} fusion(f32[2048,256]{1,0:T(8,128)} %bitcast.30, f32[256,256]{1,0:T(8,128)} %shard_map.41), kind=kOutput, calls=%fused_computation.12 | convolution fusion | flops 1610612736 | bytes 4456448 | tf_op jit(solution)/shard_map/dot_general | solution.py:10
  127.2 2.0 fusion.5
  129.2 20.6 %all_to_all.44 = f32[8,32,256]{2,1,0:T(8,128)S(1)} all-to-all(f32[8,32,256]{2,1,0:T(8,128)S(1)} %bitcast.33), channel_id=1, replica_groups=mesh['row'=64,'col'=8] {'col'}, dimensions={0} | all-to-all | bytes 524288 | tf_op jit(solution)/shard_map/all_to_all | solution.py:14
  150.6 3.4 %all-to-all-start.4 = ((f32[8,32,256]{2,1,0:T(8,128)}), f32[8,32,256]{2,1,0:T(8,128)S(1)}, u32[]{:S(2)}, u32[]{:S(2)}) async-start(f32[8,32,256]{2,1,0:T(8,128)} %broadcast_in_dim.16), calls=%async_computation.4 | async-start | bytes 524288 | tf_op jit(solution)/shard_map/all_to_all | solution.py:14
  154.4 8.6 %all-to-all-done.4 = f32[8,32,256]{2,1,0:T(8,128)S(1)} async-done(((f32[8,32,256]{2,1,0:T(8,128)}), f32[8,32,256]{2,1,0:T(8,128)S(1)}, u32[]{:S(2)}, u32[]{:S(2)}) %all-to-all-start.4) | async-done | bytes 262176 | tf_op jit(solution)/shard_map/all_to_all | solution.py:14
  163.7 1.6 all_to_all.32
  165.3 71.9 %all_to_all.45 = f32[64,1,9216]{2,1,0:T(1,128)S(1)} all-to-all(f32[64,1,9216]{2,1,0:T(1,128)S(1)} %all_to_all.32), channel_id=1, replica_groups=mesh['row'=64,'col'=8] {'row'}, dimensions={0} | all-to-all | bytes 4718592 | tf_op jit(solution)/shard_map/all_to_all | solution.py:14
  237.6 1.4 copy-done.1
  239.1 0.8 broadcast_in_dim.17
  239.9 4.5 %all-to-all-start.6 = ((f32[64,1,1024]{2,1,0:T(1,128)}), f32[64,1,1024]{2,1,0:T(1,128)S(1)}, u32[]{:S(2)}, u32[]{:S(2)}) async-start(f32[64,1,1024]{2,1,0:T(1,128)} %broadcast_in_dim.17), calls=%async_computation.6 | async-start | bytes 524288 | tf_op jit(solution)/shard_map/all_to_all | solution.py:14
  244.5 3.1 %slice.8 = f32[64,8192]{1,0:T(8,128)} slice(f32[64,9216]{1,0:T(8,128)} %bitcast.29), slice={[0:64], [0:8192]} | slice | bytes 4194304 | tf_op jit(solution)/shard_map/slice | solution.py:99
  247.5 2.7 %reshape.48 = f32[2048,256]{1,0:T(8,128)} reshape(f32[64,8192]{1,0:T(8,128)} %slice.8) | data formatting | bytes 4194304 | tf_op jit(solution)/shard_map/reshape | solution.py:99
  250.2 7.3 %all-to-all-done.6 = f32[64,1,1024]{2,1,0:T(1,128)S(1)} async-done(((f32[64,1,1024]{2,1,0:T(1,128)}), f32[64,1,1024]{2,1,0:T(1,128)S(1)}, u32[]{:S(2)}, u32[]{:S(2)}) %all-to-all-start.6) | async-done | bytes 262176 | tf_op jit(solution)/shard_map/all_to_all | solution.py:14
  258.9 3.6 %fusion = f32[2048,256]{1,0:T(8,128)S(1)} fusion(f32[2048,256]{1,0:T(8,128)} %reshape.48, f32[2048,256]{1,0:T(8,128)S(1)} %fusion.4, f32[256,256]{1,0:T(8,128)S(1)} %reshape.49), kind=kOutput, calls=%fused_computation.3 | convolution fusion | flops 1611661312 | bytes 6553600 | tf_op jit(solution)/shard_map/dot_general | solution.py:10
  262.5 3.5 %convolution_subtract_fusion.1 = f32[256,2048]{1,0:T(8,128)S(1)} fusion(f32[256,2048]{1,0:T(8,128)S(1)} %copy-done.3, f32[256,256]{1,0:T(8,128)S(1)} %fusion.3, f32[2048,256]{1,0:T(8,128)S(1)} %fusion), kind=kOutput, calls=%fused_computation.1 | convolution fusion | flops 1611137024 | bytes 6553600 | tf_op jit(solution)/shard_map/dot_general | solution.py:10
  266.1 3.3 %convolution_subtract_fusion = f32[256,2048]{1,0:T(8,128)} fusion(f32[256,2048]{1,0:T(8,128)S(1)} %convolution_subtract_fusion.1, f32[256,256]{1,0:T(8,128)S(1)} %fusion.1, f32[2048,256]{1,0:T(8,128)S(1)} %fusion.4), kind=kOutput, calls=%fused_computation | convolution fusion | flops 1611137024 | bytes 6553600 | tf_op jit(solution)/shard_map/dot_general | solution.py:10
  (31 shorter events, 5.8 us)
Async XLA Ops:
  0.6 1.0 copy-start
  27.6 17.9 %all-to-all-start.1 = ((f32[64,4,256]{2,1,0:T(4,128)}), f32[64,4,256]{2,1,0:T(4,128)S(1)}, u32[]{:S(2)}, u32[]{:S(2)}) async-start(f32[64,4,256]{2,1,0:T(4,128)} %broadcast_in_dim.12), calls=%async_computation.1 | async-start | bytes 524288 | tf_op jit(solution)/shard_map/all_to_all | solution.py:14
  47.0 75.2 %all-to-all-start.2 = ((f32[64,32,256]{2,1,0:T(8,128)}), f32[64,32,256]{2,1,0:T(8,128)S(1)}, u32[]{:S(2)}, u32[]{:S(2)}) async-start(f32[64,32,256]{2,1,0:T(8,128)} %broadcast_in_dim.13), calls=%async_computation.2 | async-start | bytes 4194304 | tf_op jit(solution)/shard_map/all_to_all | solution.py:14
  122.2 1.3 copy-start.4
  123.5 3.6 %copy-start.2 = (f32[256,2048]{1,0:T(8,128)S(1)}, f32[256,2048]{1,0:T(8,128)}, u32[]{:S(2)}) copy-start(f32[256,2048]{1,0:T(8,128)} %param.3) | copy-start | bytes 6291460
  127.1 26.8 %copy-start.5 = (f32[256,256]{1,0:T(8,128)S(1)}, f32[256,256]{1,0:T(8,128)}, u32[]{:S(2)}) copy-start(f32[256,256]{1,0:T(8,128)} %shard_map.41) | copy-start | bytes 786436
  150.6 12.5 %all-to-all-start.4 = ((f32[8,32,256]{2,1,0:T(8,128)}), f32[8,32,256]{2,1,0:T(8,128)S(1)}, u32[]{:S(2)}, u32[]{:S(2)}) async-start(f32[8,32,256]{2,1,0:T(8,128)} %broadcast_in_dim.16), calls=%async_computation.4 | async-start | bytes 524288 | tf_op jit(solution)/shard_map/all_to_all | solution.py:14
  237.6 1.4 copy-start.1
  239.9 17.6 %all-to-all-start.6 = ((f32[64,1,1024]{2,1,0:T(1,128)}), f32[64,1,1024]{2,1,0:T(1,128)S(1)}, u32[]{:S(2)}, u32[]{:S(2)}) async-start(f32[64,1,1024]{2,1,0:T(1,128)} %broadcast_in_dim.17), calls=%async_computation.6 | async-start | bytes 524288 | tf_op jit(solution)/shard_map/all_to_all | solution.py:14
  258.2 4.3 %copy-start.6 = (f32[256,256]{1,0:T(8,128)}, f32[256,256]{1,0:T(8,128)S(1)}, u32[]{:S(2)}) copy-start(f32[256,256]{1,0:T(8,128)S(1)} %reshape.49) | copy-start | bytes 786436
  258.8 3.7 %copy-start.3 = (f32[256,2048]{1,0:T(8,128)S(1)}, f32[256,2048]{1,0:T(8,128)}, u32[]{:S(2)}) copy-start(f32[256,2048]{1,0:T(8,128)} %param.3) | copy-start | bytes 6291460

commit v5 on v4

--- a/solution.py
+++ b/solution.py
@@ -47,8 +47,8 @@
         step(k, h, n)
         return c
 
-    lax.fori_loop(0, h, first, 0)
-    lax.fori_loop(h, n, second, 0)
+    lax.fori_loop(0, h, first, 0, unroll=8)
+    lax.fori_loop(h, n, second, 0, unroll=8)
     diag = jnp.sum(jnp.where(rows == cols, a_ref[...], 0.0), axis=1, keepdims=True)
     w_ref[...] = w_ref[...] / jnp.sqrt(diag)
 

time: 270 us -> 265 us (0.981)
  Pallas kernels: 69.6 us -> 64.4 us
    pallas_call x1, Pallas kernels: 69.6 us -> 64.4 us  [_inverse_cholesky(): pl.pallas_call(_inverse_cholesky_kernel, out_shape=jax.ShapeDtypeStruct((...]
  transfers between devices with their start and end apart: 4 -> 4, of which waited for: 3 -> 3; matrix products, arithmetic and copies ran while one was open for 3% -> 3% of each run, Pallas kernels for 26% -> 24%
where the time goes in v5:
time: 265 us; the launch traced here: 264 us
  blocking collectives  117 us (44%)
  Pallas kernels  64.4 us (24%)
  waiting for transfers between devices  28.8 us (11%)
  matrix products  18.1 us (7%)
  starting transfers between devices  17.7 us (7%)
  local copies, waits for them, and re-layouts  16.4 us (6%)
    all_to_all x3, blocking collectives, _exchange(): return lax.all_to_all(x, axis, 0, 0, tiled=False)  117 us
    pallas_call x1, Pallas kernels, _inverse_cholesky(): pl.pallas_call(_inverse_cholesky_kernel, out_shape=jax.ShapeDtypeStruct((...  64.4 us
    all_to_all x4, waiting for transfers between devices, _exchange(): return lax.all_to_all(x, axis, 0, 0, tiled=False)  28.8 us
    dot_general x9, matrix products, _dot(): return jnp.dot(a, b, precision=lax.Precision.HIGHEST)  18.1 us
    all_to_all x4, starting transfers between devices, _exchange(): return lax.all_to_all(x, axis, 0, 0, tiled=False)  17.7 us
  transfers between devices with their start and end apart: 4, of which 3 were waited for; matrix products, arithmetic and copies ran while one was open for 3% of the time, Pallas kernels for 24%

profile of v5, /device:TPU:1, one launch (start us, length us, event | category | flops | bytes accessed | tf_op | source)
XLA Modules:
  0.0 264.1 jit_solution(2648560917308450459)
XLA Ops:
  0.6 0.9 copy-done
  2.3 24.5 %all_to_all.43 = f32[64,4,256]{2,1,0:T(4,128)S(1)} all-to-all(f32[64,4,256]{2,1,0:T(4,128)S(1)} %reshape.42), channel_id=1, replica_groups=mesh['row'=64,'col'=8] {'row'}, dimensions={0} | all-to-all | bytes 524288 | tf_op jit(solution)/shard_map/all_to_all | solution.py:14
  27.6 4.8 %all-to-all-start.1 = ((f32[64,4,256]{2,1,0:T(4,128)}), f32[64,4,256]{2,1,0:T(4,128)S(1)}, u32[]{:S(2)}, u32[]{:S(2)}) async-start(f32[64,4,256]{2,1,0:T(4,128)} %broadcast_in_dim.12), calls=%async_computation.1 | async-start | bytes 524288 | tf_op jit(solution)/shard_map/all_to_all | solution.py:14
  32.4 13.1 %all-to-all-done.1 = f32[64,4,256]{2,1,0:T(4,128)S(1)} async-done(((f32[64,4,256]{2,1,0:T(4,128)}), f32[64,4,256]{2,1,0:T(4,128)S(1)}, u32[]{:S(2)}, u32[]{:S(2)}) %all-to-all-start.1) | async-done | bytes 262176 | tf_op jit(solution)/shard_map/all_to_all | solution.py:14
  45.4 1.6 broadcast_in_dim.13
  47.0 4.8 %all-to-all-start.2 = ((f32[64,32,256]{2,1,0:T(8,128)}), f32[64,32,256]{2,1,0:T(8,128)S(1)}, u32[]{:S(2)}, u32[]{:S(2)}) async-start(f32[64,32,256]{2,1,0:T(8,128)} %broadcast_in_dim.13), calls=%async_computation.2 | async-start | bytes 4194304 | tf_op jit(solution)/shard_map/all_to_all | solution.py:14
  52.6 64.4 %shard_map.41 = f32[256,256]{1,0:T(8,128)} custom-call(f32[256,256]{1,0:T(8,128)} %reshape.43.g_ref), custom_call_target="tpu_custom_call" | custom-call | flops 33554432 | bytes 524288 | tf_op jit(solution)/shard_map/pallas_call | solution.py:58
  117.0 1.3 copy-done.4
  118.3 3.6 %fusion.4 = f32[2048,256]{1,0:T(8,128)S(1)} fusion(f32[2048,256]{1,0:T(8,128)} %bitcast.30, f32[256,256]{1,0:T(8,128)} %shard_map.41), kind=kOutput, calls=%fused_computation.12 | convolution fusion | flops 1610612736 | bytes 4456448 | tf_op jit(solution)/shard_map/dot_general | solution.py:10
  121.9 2.0 fusion.5
  123.9 20.6 %all_to_all.44 = f32[8,32,256]{2,1,0:T(8,128)S(1)} all-to-all(f32[8,32,256]{2,1,0:T(8,128)S(1)} %bitcast.33), channel_id=1, replica_groups=mesh['row'=64,'col'=8] {'col'}, dimensions={0} | all-to-all | bytes 524288 | tf_op jit(solution)/shard_map/all_to_all | solution.py:14
  145.3 3.6 %all-to-all-start.4 = ((f32[8,32,256]{2,1,0:T(8,128)}), f32[8,32,256]{2,1,0:T(8,128)S(1)}, u32[]{:S(2)}, u32[]{:S(2)}) async-start(f32[8,32,256]{2,1,0:T(8,128)} %broadcast_in_dim.16), calls=%async_computation.4 | async-start | bytes 524288 | tf_op jit(solution)/shard_map/all_to_all | solution.py:14
  149.3 8.5 %all-to-all-done.4 = f32[8,32,256]{2,1,0:T(8,128)S(1)} async-done(((f32[8,32,256]{2,1,0:T(8,128)}), f32[8,32,256]{2,1,0:T(8,128)S(1)}, u32[]{:S(2)}, u32[]{:S(2)}) %all-to-all-start.4) | async-done | bytes 262176 | tf_op jit(solution)/shard_map/all_to_all | solution.py:14
  158.5 1.6 all_to_all.32
  160.1 71.8 %all_to_all.45 = f32[64,1,9216]{2,1,0:T(1,128)S(1)} all-to-all(f32[64,1,9216]{2,1,0:T(1,128)S(1)} %all_to_all.32), channel_id=1, replica_groups=mesh['row'=64,'col'=8] {'row'}, dimensions={0} | all-to-all | bytes 4718592 | tf_op jit(solution)/shard_map/all_to_all | solution.py:14
  232.3 1.4 copy-done.1
  233.8 0.8 broadcast_in_dim.17
  234.6 4.5 %all-to-all-start.6 = ((f32[64,1,1024]{2,1,0:T(1,128)}), f32[64,1,1024]{2,1,0:T(1,128)S(1)}, u32[]{:S(2)}, u32[]{:S(2)}) async-start(f32[64,1,1024]{2,1,0:T(1,128)} %broadcast_in_dim.17), calls=%async_computation.6 | async-start | bytes 524288 | tf_op jit(solution)/shard_map/all_to_all | solution.py:14
  239.2 3.1 %slice.8 = f32[64,8192]{1,0:T(8,128)} slice(f32[64,9216]{1,0:T(8,128)} %bitcast.29), slice={[0:64], [0:8192]} | slice | bytes 4194304 | tf_op jit(solution)/shard_map/slice | solution.py:99
  242.2 2.7 %reshape.48 = f32[2048,256]{1,0:T(8,128)} reshape(f32[64,8192]{1,0:T(8,128)} %slice.8) | data formatting | bytes 4194304 | tf_op jit(solution)/shard_map/reshape | solution.py:99
  245.0 7.3 %all-to-all-done.6 = f32[64,1,1024]{2,1,0:T(1,128)S(1)} async-done(((f32[64,1,1024]{2,1,0:T(1,128)}), f32[64,1,1024]{2,1,0:T(1,128)S(1)}, u32[]{:S(2)}, u32[]{:S(2)}) %all-to-all-start.6) | async-done | bytes 262176 | tf_op jit(solution)/shard_map/all_to_all | solution.py:14
  253.6 3.6 %fusion = f32[2048,256]{1,0:T(8,128)S(1)} fusion(f32[2048,256]{1,0:T(8,128)} %reshape.48, f32[2048,256]{1,0:T(8,128)S(1)} %fusion.4, f32[256,256]{1,0:T(8,128)S(1)} %reshape.49), kind=kOutput, calls=%fused_computation.3 | convolution fusion | flops 1611661312 | bytes 6553600 | tf_op jit(solution)/shard_map/dot_general | solution.py:10
  257.2 3.5 %convolution_subtract_fusion.1 = f32[256,2048]{1,0:T(8,128)S(1)} fusion(f32[256,2048]{1,0:T(8,128)S(1)} %copy-done.3, f32[256,256]{1,0:T(8,128)S(1)} %fusion.3, f32[2048,256]{1,0:T(8,128)S(1)} %fusion), kind=kOutput, calls=%fused_computation.1 | convolution fusion | flops 1611137024 | bytes 6553600 | tf_op jit(solution)/shard_map/dot_general | solution.py:10
  260.8 3.4 %convolution_subtract_fusion = f32[256,2048]{1,0:T(8,128)} fusion(f32[256,2048]{1,0:T(8,128)S(1)} %convolution_subtract_fusion.1, f32[256,256]{1,0:T(8,128)S(1)} %fusion.1, f32[2048,256]{1,0:T(8,128)S(1)} %fusion.4), kind=kOutput, calls=%fused_computation | convolution fusion | flops 1611137024 | bytes 6553600 | tf_op jit(solution)/shard_map/dot_general | solution.py:10
  (31 shorter events, 5.9 us)
Async XLA Ops:
  0.6 1.0 copy-start
  27.6 17.9 %all-to-all-start.1 = ((f32[64,4,256]{2,1,0:T(4,128)}), f32[64,4,256]{2,1,0:T(4,128)S(1)}, u32[]{:S(2)}, u32[]{:S(2)}) async-start(f32[64,4,256]{2,1,0:T(4,128)} %broadcast_in_dim.12), calls=%async_computation.1 | async-start | bytes 524288 | tf_op jit(solution)/shard_map/all_to_all | solution.py:14
  47.0 69.9 %all-to-all-start.2 = ((f32[64,32,256]{2,1,0:T(8,128)}), f32[64,32,256]{2,1,0:T(8,128)S(1)}, u32[]{:S(2)}, u32[]{:S(2)}) async-start(f32[64,32,256]{2,1,0:T(8,128)} %broadcast_in_dim.13), calls=%async_computation.2 | async-start | bytes 4194304 | tf_op jit(solution)/shard_map/all_to_all | solution.py:14
  117.0 1.3 copy-start.4
  118.3 3.6 %copy-start.2 = (f32[256,2048]{1,0:T(8,128)S(1)}, f32[256,2048]{1,0:T(8,128)}, u32[]{:S(2)}) copy-start(f32[256,2048]{1,0:T(8,128)} %param.3) | copy-start | bytes 6291460
  121.9 27.0 %copy-start.5 = (f32[256,256]{1,0:T(8,128)S(1)}, f32[256,256]{1,0:T(8,128)}, u32[]{:S(2)}) copy-start(f32[256,256]{1,0:T(8,128)} %shard_map.41) | copy-start | bytes 786436
  145.3 12.6 %all-to-all-start.4 = ((f32[8,32,256]{2,1,0:T(8,128)}), f32[8,32,256]{2,1,0:T(8,128)S(1)}, u32[]{:S(2)}, u32[]{:S(2)}) async-start(f32[8,32,256]{2,1,0:T(8,128)} %broadcast_in_dim.16), calls=%async_computation.4 | async-start | bytes 524288 | tf_op jit(solution)/shard_map/all_to_all | solution.py:14
  232.3 1.4 copy-start.1
  234.6 17.6 %all-to-all-start.6 = ((f32[64,1,1024]{2,1,0:T(1,128)}), f32[64,1,1024]{2,1,0:T(1,128)S(1)}, u32[]{:S(2)}, u32[]{:S(2)}) async-start(f32[64,1,1024]{2,1,0:T(1,128)} %broadcast_in_dim.17), calls=%async_computation.6 | async-start | bytes 524288 | tf_op jit(solution)/shard_map/all_to_all | solution.py:14
  252.9 4.3 %copy-start.6 = (f32[256,256]{1,0:T(8,128)}, f32[256,256]{1,0:T(8,128)S(1)}, u32[]{:S(2)}) copy-start(f32[256,256]{1,0:T(8,128)S(1)} %reshape.49) | copy-start | bytes 786436
  253.6 3.7 %copy-start.3 = (f32[256,2048]{1,0:T(8,128)S(1)}, f32[256,2048]{1,0:T(8,128)}, u32[]{:S(2)}) copy-start(f32[256,2048]{1,0:T(8,128)} %param.3) | copy-start | bytes 6291460

commit v6 on v3

--- a/solution.py
+++ b/solution.py
@@ -50,14 +50,14 @@
 
     send = jnp.concatenate(
         [
-            jnp.broadcast_to(own_moment.reshape(1, piece * k), (n_row, piece * k)),
-            band_part.reshape(n_row, (k // n_row) * k),
+            jnp.broadcast_to(own_moment[None], (n_row, piece, k)),
+            band_part.reshape(n_row, k // n_row, k),
         ],
         axis=1,
     )
     got = _exchange(send, "row")
-    moment_stored = got[:, : piece * k].reshape(n_row * piece, k)
-    band_rows = got[:, piece * k :].sum(0)
+    moment_stored = got[:, :piece].reshape(n_row * piece, k)
+    band_rows = got[:, piece:].sum(0)
     band_block = _exchange(jnp.broadcast_to(band_rows[None], (n_row,) + band_rows.shape), "row").reshape(k, k)
 
     corrected_own = moment_own - 0.5 * _dot(basis_own, band_block)

time: 248 us -> 251 us (1.012)
  blocking collectives: 115 us -> 120 us
  local copies, waits for them, and re-layouts: 16.1 us -> 11.9 us
    all_to_all x3, blocking collectives: 115 us -> 120 us  [_exchange(): return lax.all_to_all(x, axis, 0, 0, tiled=False)]
    reshape x2 -> x0, local copies, waits for them, and re-layouts: 2.81 us -> none  [the longest x1 2.74 us: shards(): moment_stored = got[:, :piece * k].reshape(n_row * piece, k)]
    all_to_all x4, waiting for transfers between devices: 30.7 us -> 33.2 us  [_exchange(): return lax.all_to_all(x, axis, 0, 0, tiled=False)]
  transfers between devices with their start and end apart: 4 -> 4, of which waited for: 4 -> 4; matrix products, arithmetic and copies ran while one was open for 22% -> 21% of each run, Pallas kernels for 0% -> 0%
where the time goes in v6:
time: 251 us
  blocking collectives  120 us (48%)
  other arithmetic  46.4 us (18%)
  waiting for transfers between devices  33.2 us (13%)
  matrix products  19.7 us (8%)
  starting transfers between devices  18.7 us (7%)
  local copies, waits for them, and re-layouts  11.9 us (5%)
    all_to_all x3, blocking collectives, _exchange(): return lax.all_to_all(x, axis, 0, 0, tiled=False)  120 us
    all_to_all x4, waiting for transfers between devices, _exchange(): return lax.all_to_all(x, axis, 0, 0, tiled=False)  33.2 us
    dot_general x13, matrix products, _dot(): return jnp.dot(a, b, precision=lax.Precision.HIGHEST)  19.1 us
    all_to_all x4, starting transfers between devices, _exchange(): return lax.all_to_all(x, axis, 0, 0, tiled=False)  18.7 us
    another operation x3, other arithmetic, _inverse_cholesky(): l11 = jnp.linalg.cholesky(gram[:h, :h])  12.4 us
    another operation x3, other arithmetic, _inverse_cholesky(): l22 = jnp.linalg.cholesky(gram[h:, h:] - _dot(l21, l21.T))  12.4 us
    another operation x2, other arithmetic, _inverse_cholesky(): i22 = jax.scipy.linalg.solve_triangular(l22, eye, lower=True)  10.6 us
    another operation x2, other arithmetic, _inverse_cholesky(): i11 = jax.scipy.linalg.solve_triangular(l11, eye, lower=True)  10.5 us
  transfers between devices with their start and end apart: 4, of which 4 were waited for; matrix products, arithmetic and copies ran while one was open for 21% of the time, Pallas kernels for 0%

profile of v6, /device:TPU:1, one launch (start us, length us, event | category | flops | bytes accessed | tf_op | source)
XLA Modules:
  0.0 250.6 jit_solution(14016315902828475511)
XLA Ops:
  2.3 24.5 %all_to_all.35 = f32[64,4,256]{2,1,0:T(4,128)S(1)} all-to-all(f32[64,4,256]{2,1,0:T(4,128)S(1)} %reshape.39), channel_id=1, replica_groups=mesh['row'=64,'col'=8] {'row'}, dimensions={0} | all-to-all | bytes 524288 | tf_op jit(solution)/shard_map/all_to_all | solution.py:12
  27.6 4.8 %all-to-all-start.1 = ((f32[64,4,256]{2,1,0:T(4,128)}), f32[64,4,256]{2,1,0:T(4,128)S(1)}, u32[]{:S(2)}, u32[]{:S(2)}) async-start(f32[64,4,256]{2,1,0:T(4,128)} %broadcast_in_dim.11), calls=%async_computation.1 | async-start | bytes 524288 | tf_op jit(solution)/shard_map/all_to_all | solution.py:12
  32.4 13.1 %all-to-all-done.1 = f32[64,4,256]{2,1,0:T(4,128)S(1)} async-done(((f32[64,4,256]{2,1,0:T(4,128)}), f32[64,4,256]{2,1,0:T(4,128)S(1)}, u32[]{:S(2)}, u32[]{:S(2)}) %all-to-all-start.1) | async-done | bytes 262176 | tf_op jit(solution)/shard_map/all_to_all | solution.py:12
  45.4 1.6 broadcast_in_dim.12
  47.0 5.0 %all-to-all-start.2 = ((f32[64,32,256]{2,1,0:T(8,128)}), f32[64,32,256]{2,1,0:T(8,128)S(1)}, u32[]{:S(2)}, u32[]{:S(2)}) async-start(f32[64,32,256]{2,1,0:T(8,128)} %broadcast_in_dim.12), calls=%async_computation.2 | async-start | bytes 4194304 | tf_op jit(solution)/shard_map/all_to_all | solution.py:12
  52.3 11.7 %cholesky.44 = f32[128,128]{1,0:T(8,128)S(1)} custom-call(f32[128,128]{1,0:T(8,128)S(1)} %get-tuple-element.5), custom_call_target="Cholesky" | custom-call | tf_op jit(solution)/shard_map/jit(cholesky)/cholesky | solution.py:18
  65.4 9.8 %custom-call.6 = f32[1,128,128]{1,2,0:T(8,128)S(1)} custom-call(f32[1,128,128]{2,1,0:T(8,128)S(1)} %fusion.14), custom_call_target="InvertDiagBlocksLowerTriangular" | custom-call | tf_op jit(solution)/shard_map/jit(_solve_triangular)/triangular_solve | solution.py:19
  76.1 11.7 %cholesky.55 = f32[128,128]{1,0:T(8,128)S(1)} custom-call(f32[128,128]{1,0:T(8,128)S(1)} %fusion.19), custom_call_target="Cholesky" | custom-call | tf_op jit(solution)/shard_map/jit(cholesky)/cholesky | solution.py:21
  89.2 10.0 %custom-call.7 = f32[1,128,128]{1,2,0:T(8,128)S(1)} custom-call(f32[1,128,128]{2,1,0:T(8,128)S(1)} %fusion.15), custom_call_target="InvertDiagBlocksLowerTriangular" | custom-call | tf_op jit(solution)/shard_map/jit(_solve_triangular)/triangular_solve | solution.py:22
  100.1 1.4 all-to-all-done.2
  101.5 1.3 copy-done.4
  102.8 3.6 %fusion.4 = f32[2048,256]{1,0:T(8,128)S(1)} fusion(f32[2048,256]{1,0:T(8,128)} %bitcast.49, f32[128,128]{1,0:T(8,128)S(1)} %fusion.12, f32[128,128]{1,0:T(8,128)S(1)} %copy.35, f32[128,128]{1,0:T(8,128)S(1)} %convolution_negate_fusion), kind=kOutput, calls=%fused_computation.14 | convolution fusion | flops 1610874880 | bytes 4390912 | tf_op jit(solution)/shard_map/dot_general | solution.py:8
  106.4 2.0 fusion.31
  108.4 19.3 %all_to_all.36 = f32[8,32,256]{2,1,0:T(8,128)S(1)} all-to-all(f32[8,32,256]{2,1,0:T(8,128)S(1)} %bitcast.52), channel_id=1, replica_groups=mesh['row'=64,'col'=8] {'col'}, dimensions={0} | all-to-all | bytes 524288 | tf_op jit(solution)/shard_map/all_to_all | solution.py:12
  128.4 3.4 %all-to-all-start.4 = ((f32[8,32,256]{2,1,0:T(8,128)}), f32[8,32,256]{2,1,0:T(8,128)S(1)}, u32[]{:S(2)}, u32[]{:S(2)}) async-start(f32[8,32,256]{2,1,0:T(8,128)} %broadcast_in_dim.14), calls=%async_computation.4 | async-start | bytes 524288 | tf_op jit(solution)/shard_map/all_to_all | solution.py:12
  132.4 8.8 %all-to-all-done.4 = f32[8,32,256]{2,1,0:T(8,128)S(1)} async-done(((f32[8,32,256]{2,1,0:T(8,128)}), f32[8,32,256]{2,1,0:T(8,128)S(1)}, u32[]{:S(2)}, u32[]{:S(2)}) %all-to-all-start.4) | async-done | bytes 262176 | tf_op jit(solution)/shard_map/all_to_all | solution.py:12
  142.3 76.0 %all_to_all.37 = f32[64,36,256]{2,1,0:T(8,128)S(1)} all-to-all(f32[64,36,256]{2,1,0:T(8,128)S(1)} %pad_maximum_fusion), channel_id=1, replica_groups=mesh['row'=64,'col'=8] {'row'}, dimensions={0} | all-to-all | bytes 4718592 | tf_op jit(solution)/shard_map/all_to_all | solution.py:12
  218.3 1.5 copy-done.1
  220.6 5.6 %all-to-all-start.6 = ((f32[64,4,256]{2,1,0:T(4,128)}), f32[64,4,256]{2,1,0:T(4,128)S(1)}, u32[]{:S(2)}, u32[]{:S(2)}) async-start(f32[64,4,256]{2,1,0:T(4,128)} %broadcast_in_dim.15), calls=%async_computation.6 | async-start | bytes 524288 | tf_op jit(solution)/shard_map/all_to_all | solution.py:12
  226.3 3.2 %slice.31 = f32[64,32,256]{2,1,0:T(8,128)} slice(f32[64,36,256]{2,1,0:T(8,128)} %copy-done.1), slice={[0:64], [0:32], [0:256]} | slice | bytes 4194304 | tf_op jit(solution)/shard_map/slice | solution.py:59
  229.4 9.9 %all-to-all-done.6 = f32[64,4,256]{2,1,0:T(4,128)S(1)} async-done(((f32[64,4,256]{2,1,0:T(4,128)}), f32[64,4,256]{2,1,0:T(4,128)S(1)}, u32[]{:S(2)}, u32[]{:S(2)}) %all-to-all-start.6) | async-done | bytes 262176 | tf_op jit(solution)/shard_map/all_to_all | solution.py:12
  240.0 3.6 %fusion = f32[2048,256]{1,0:T(8,128)S(1)} fusion(f32[2048,256]{1,0:T(8,128)} %bitcast.48, f32[2048,256]{1,0:T(8,128)S(1)} %fusion.4, f32[256,256]{1,0:T(8,128)S(1)} %reshape.45), kind=kOutput, calls=%fused_computation.3 | convolution fusion | flops 1611661312 | bytes 6553600 | tf_op jit(solution)/shard_map/dot_general | solution.py:8
  243.7 3.5 %convolution_subtract_fusion.1 = f32[256,2048]{1,0:T(8,128)S(1)} fusion(f32[256,2048]{1,0:T(8,128)S(1)} %copy-done.3, f32[256,256]{1,0:T(8,128)S(1)} %fusion.5, f32[2048,256]{1,0:T(8,128)S(1)} %fusion), kind=kOutput, calls=%fused_computation.1 | convolution fusion | flops 1611137024 | bytes 6553600 | tf_op jit(solution)/shard_map/dot_general | solution.py:8
  247.3 3.4 %convolution_subtract_fusion = f32[256,2048]{1,0:T(8,128)} fusion(f32[256,2048]{1,0:T(8,128)S(1)} %convolution_subtract_fusion.1, f32[256,256]{1,0:T(8,128)S(1)} %fusion.1, f32[2048,256]{1,0:T(8,128)S(1)} %fusion.4), kind=kOutput, calls=%fused_computation | convolution fusion | flops 1611137024 | bytes 6553600 | tf_op jit(solution)/shard_map/dot_general | solution.py:8
  (47 shorter events, 11.0 us)
Async XLA Ops:
  0.6 1.0 copy-start
  27.6 17.9 %all-to-all-start.1 = ((f32[64,4,256]{2,1,0:T(4,128)}), f32[64,4,256]{2,1,0:T(4,128)S(1)}, u32[]{:S(2)}, u32[]{:S(2)}) async-start(f32[64,4,256]{2,1,0:T(4,128)} %broadcast_in_dim.11), calls=%async_computation.1 | async-start | bytes 524288 | tf_op jit(solution)/shard_map/all_to_all | solution.py:12
  47.0 54.5 %all-to-all-start.2 = ((f32[64,32,256]{2,1,0:T(8,128)}), f32[64,32,256]{2,1,0:T(8,128)S(1)}, u32[]{:S(2)}, u32[]{:S(2)}) async-start(f32[64,32,256]{2,1,0:T(8,128)} %broadcast_in_dim.12), calls=%async_computation.2 | async-start | bytes 4194304 | tf_op jit(solution)/shard_map/all_to_all | solution.py:12
  101.5 1.3 copy-start.4
  102.8 3.6 %copy-start.2 = (f32[256,2048]{1,0:T(8,128)S(1)}, f32[256,2048]{1,0:T(8,128)}, u32[]{:S(2)}) copy-start(f32[256,2048]{1,0:T(8,128)} %param.6) | copy-start | bytes 6291460
  128.4 12.8 %all-to-all-start.4 = ((f32[8,32,256]{2,1,0:T(8,128)}), f32[8,32,256]{2,1,0:T(8,128)S(1)}, u32[]{:S(2)}, u32[]{:S(2)}) async-start(f32[8,32,256]{2,1,0:T(8,128)} %broadcast_in_dim.14), calls=%async_computation.4 | async-start | bytes 524288 | tf_op jit(solution)/shard_map/all_to_all | solution.py:12
  218.3 1.5 copy-start.1
  220.6 18.7 %all-to-all-start.6 = ((f32[64,4,256]{2,1,0:T(4,128)}), f32[64,4,256]{2,1,0:T(4,128)S(1)}, u32[]{:S(2)}, u32[]{:S(2)}) async-start(f32[64,4,256]{2,1,0:T(4,128)} %broadcast_in_dim.15), calls=%async_computation.6 | async-start | bytes 524288 | tf_op jit(solution)/shard_map/all_to_all | solution.py:12
  239.4 4.3 %copy-start.5 = (f32[256,256]{1,0:T(8,128)}, f32[256,256]{1,0:T(8,128)S(1)}, u32[]{:S(2)}) copy-start(f32[256,256]{1,0:T(8,128)S(1)} %reshape.45) | copy-start | bytes 786436
  240.0 3.7 %copy-start.3 = (f32[256,2048]{1,0:T(8,128)S(1)}, f32[256,2048]{1,0:T(8,128)}, u32[]{:S(2)}) copy-start(f32[256,2048]{1,0:T(8,128)} %param.6) | copy-start | bytes 6291460

commit v7 on v5

--- a/solution.py
+++ b/solution.py
@@ -16,39 +16,42 @@
 
 def _inverse_cholesky_kernel(g_ref, w_ref, a_ref):
     n = g_ref.shape[0]
-    h = n // 2
     rows = lax.broadcasted_iota(jnp.int32, (n, n), 0)
     cols = lax.broadcasted_iota(jnp.int32, (n, n), 1)
     a_ref[...] = g_ref[...]
     w_ref[...] = jnp.where(rows == cols, 1.0, 0.0).astype(w_ref.dtype)
-    lane = lax.broadcasted_iota(jnp.int32, (1, n), 1)
+    lane = lax.broadcasted_iota(jnp.int32, (8, n), 1)
+    sub = lax.broadcasted_iota(jnp.int32, (8, 1), 0)
 
-    sub = lax.broadcasted_iota(jnp.int32, (8, n), 0)
+    def block(b, carry):
+        k0 = pl.multiple_of(b * 8, 8)
+        r = a_ref[pl.ds(k0, 8), :]
+        wb = w_ref[pl.ds(k0, 8), :]
+        scale = jnp.zeros((8, 1), r.dtype)
+        for s in range(8):
+            k = k0 + s
+            row = r[s : s + 1, :]
+            piv = jnp.sum(jnp.where(lane[0:1] == k, row, 0.0))
+            col = jnp.sum(jnp.where(lane == k, r, 0.0), axis=1, keepdims=True)
+            fb = jnp.where(sub > s, col / piv, 0.0)
+            r = r - fb * row
+            wb = wb - fb * wb[s : s + 1, :]
+            scale = jnp.where(sub == s, 1.0 / piv, scale)
+        f = jnp.where(lane >= k0 + 8, r * scale, 0.0).T
+        a_ref[pl.ds(k0, 8), :] = r
+        w_ref[pl.ds(k0, 8), :] = wb
+        for c0 in range(0, n, 32):
+            fc = f[c0 : c0 + 32, :]
+            upd_a = a_ref[c0 : c0 + 32, :]
+            upd_w = w_ref[c0 : c0 + 32, :]
+            for s in range(8):
+                upd_a = upd_a - fc[:, s : s + 1] * r[s : s + 1, :]
+                upd_w = upd_w - fc[:, s : s + 1] * wb[s : s + 1, :]
+            a_ref[c0 : c0 + 32, :] = upd_a
+            w_ref[c0 : c0 + 32, :] = upd_w
+        return carry
 
-    def row_of(ref, k, width):
-        base = pl.multiple_of((k // 8) * 8, 8)
-        block = ref[pl.ds(base, 8), :width]
-        return jnp.sum(jnp.where(sub[:, :width] == k - base, block, 0.0), axis=0, keepdims=True)
-
-    def step(k, lo, w_cols):
-        row_a = row_of(a_ref, k, n)
-        piv = jnp.sum(jnp.where(lane == k, row_a, 0.0))
-        col = jnp.broadcast_to(row_a, (8, n)).T[lo:, 0:1]
-        ridx = lax.broadcasted_iota(jnp.int32, (n - lo, 1), 0) + lo
-        f = jnp.where(ridx > k, col / piv, 0.0)
-        a_ref[lo:, lo:] = a_ref[lo:, lo:] - f * row_a[:, lo:]
-        w_ref[lo:, :w_cols] = w_ref[lo:, :w_cols] - f * row_of(w_ref, k, w_cols)
-
-    def first(k, c):
-        step(k, 0, h)
-        return c
-
-    def second(k, c):
-        step(k, h, n)
-        return c
-
-    lax.fori_loop(0, h, first, 0, unroll=8)
-    lax.fori_loop(h, n, second, 0, unroll=8)
+    lax.fori_loop(0, n // 8, block, 0)
     diag = jnp.sum(jnp.where(rows == cols, a_ref[...], 0.0), axis=1, keepdims=True)
     w_ref[...] = w_ref[...] / jnp.sqrt(diag)
 

time: 265 us -> 254 us (0.958)
  Pallas kernels: 64.4 us -> 53.5 us
    pallas_call x1, Pallas kernels: 64.4 us -> 53.5 us  [_inverse_cholesky(): pl.pallas_call(_inverse_cholesky_kernel, out_shape=jax.ShapeDtypeStruct((...]
  transfers between devices with their start and end apart: 4 -> 4, of which waited for: 3 -> 3; matrix products, arithmetic and copies ran while one was open for 3% -> 3% of each run, Pallas kernels for 24% -> 21%
where the time goes in v7:
time: 254 us; the launch traced here: 253 us
  blocking collectives  117 us (46%)
  Pallas kernels  53.5 us (21%)
  waiting for transfers between devices  29 us (11%)
  matrix products  18.1 us (7%)
  starting transfers between devices  17.5 us (7%)
  local copies, waits for them, and re-layouts  16.4 us (6%)
    all_to_all x3, blocking collectives, _exchange(): return lax.all_to_all(x, axis, 0, 0, tiled=False)  117 us
    pallas_call x1, Pallas kernels, _inverse_cholesky(): pl.pallas_call(_inverse_cholesky_kernel, out_shape=jax.ShapeDtypeStruct((...  53.5 us
    all_to_all x4, waiting for transfers between devices, _exchange(): return lax.all_to_all(x, axis, 0, 0, tiled=False)  29 us
    dot_general x9, matrix products, _dot(): return jnp.dot(a, b, precision=lax.Precision.HIGHEST)  18.1 us
    all_to_all x4, starting transfers between devices, _exchange(): return lax.all_to_all(x, axis, 0, 0, tiled=False)  17.5 us
  transfers between devices with their start and end apart: 4, of which 3 were waited for; matrix products, arithmetic and copies ran while one was open for 3% of the time, Pallas kernels for 21%

profile of v7, /device:TPU:1, one launch (start us, length us, event | category | flops | bytes accessed | tf_op | source)
XLA Modules:
  0.0 253.4 jit_solution(15047397257586166131)
XLA Ops:
  0.6 0.9 copy-done
  2.3 24.5 %all_to_all.43 = f32[64,4,256]{2,1,0:T(4,128)S(1)} all-to-all(f32[64,4,256]{2,1,0:T(4,128)S(1)} %reshape.42), channel_id=1, replica_groups=mesh['row'=64,'col'=8] {'row'}, dimensions={0} | all-to-all | bytes 524288 | tf_op jit(solution)/shard_map/all_to_all | solution.py:14
  27.6 4.8 %all-to-all-start.1 = ((f32[64,4,256]{2,1,0:T(4,128)}), f32[64,4,256]{2,1,0:T(4,128)S(1)}, u32[]{:S(2)}, u32[]{:S(2)}) async-start(f32[64,4,256]{2,1,0:T(4,128)} %broadcast_in_dim.12), calls=%async_computation.1 | async-start | bytes 524288 | tf_op jit(solution)/shard_map/all_to_all | solution.py:14
  32.4 13.1 %all-to-all-done.1 = f32[64,4,256]{2,1,0:T(4,128)S(1)} async-done(((f32[64,4,256]{2,1,0:T(4,128)}), f32[64,4,256]{2,1,0:T(4,128)S(1)}, u32[]{:S(2)}, u32[]{:S(2)}) %all-to-all-start.1) | async-done | bytes 262176 | tf_op jit(solution)/shard_map/all_to_all | solution.py:14
  45.4 1.6 broadcast_in_dim.13
  47.0 4.8 %all-to-all-start.2 = ((f32[64,32,256]{2,1,0:T(8,128)}), f32[64,32,256]{2,1,0:T(8,128)S(1)}, u32[]{:S(2)}, u32[]{:S(2)}) async-start(f32[64,32,256]{2,1,0:T(8,128)} %broadcast_in_dim.13), calls=%async_computation.2 | async-start | bytes 4194304 | tf_op jit(solution)/shard_map/all_to_all | solution.py:14
  52.6 53.5 %shard_map.41 = f32[256,256]{1,0:T(8,128)} custom-call(f32[256,256]{1,0:T(8,128)} %reshape.43.g_ref), custom_call_target="tpu_custom_call" | custom-call | flops 33554432 | bytes 524288 | tf_op jit(solution)/shard_map/pallas_call | solution.py:61
  106.1 1.3 copy-done.4
  107.4 3.6 %fusion.4 = f32[2048,256]{1,0:T(8,128)S(1)} fusion(f32[2048,256]{1,0:T(8,128)} %bitcast.30, f32[256,256]{1,0:T(8,128)} %shard_map.41), kind=kOutput, calls=%fused_computation.12 | convolution fusion | flops 1610612736 | bytes 4456448 | tf_op jit(solution)/shard_map/dot_general | solution.py:10
  111.0 2.0 fusion.5
  113.0 20.6 %all_to_all.44 = f32[8,32,256]{2,1,0:T(8,128)S(1)} all-to-all(f32[8,32,256]{2,1,0:T(8,128)S(1)} %bitcast.33), channel_id=1, replica_groups=mesh['row'=64,'col'=8] {'col'}, dimensions={0} | all-to-all | bytes 524288 | tf_op jit(solution)/shard_map/all_to_all | solution.py:14
  134.4 3.4 %all-to-all-start.4 = ((f32[8,32,256]{2,1,0:T(8,128)}), f32[8,32,256]{2,1,0:T(8,128)S(1)}, u32[]{:S(2)}, u32[]{:S(2)}) async-start(f32[8,32,256]{2,1,0:T(8,128)} %broadcast_in_dim.16), calls=%async_computation.4 | async-start | bytes 524288 | tf_op jit(solution)/shard_map/all_to_all | solution.py:14
  138.3 8.6 %all-to-all-done.4 = f32[8,32,256]{2,1,0:T(8,128)S(1)} async-done(((f32[8,32,256]{2,1,0:T(8,128)}), f32[8,32,256]{2,1,0:T(8,128)S(1)}, u32[]{:S(2)}, u32[]{:S(2)}) %all-to-all-start.4) | async-done | bytes 262176 | tf_op jit(solution)/shard_map/all_to_all | solution.py:14
  147.5 1.6 all_to_all.32
  149.2 72.0 %all_to_all.45 = f32[64,1,9216]{2,1,0:T(1,128)S(1)} all-to-all(f32[64,1,9216]{2,1,0:T(1,128)S(1)} %all_to_all.32), channel_id=1, replica_groups=mesh['row'=64,'col'=8] {'row'}, dimensions={0} | all-to-all | bytes 4718592 | tf_op jit(solution)/shard_map/all_to_all | solution.py:14
  221.6 1.4 copy-done.1
  223.1 0.8 broadcast_in_dim.17
  223.9 4.5 %all-to-all-start.6 = ((f32[64,1,1024]{2,1,0:T(1,128)}), f32[64,1,1024]{2,1,0:T(1,128)S(1)}, u32[]{:S(2)}, u32[]{:S(2)}) async-start(f32[64,1,1024]{2,1,0:T(1,128)} %broadcast_in_dim.17), calls=%async_computation.6 | async-start | bytes 524288 | tf_op jit(solution)/shard_map/all_to_all | solution.py:14
  228.5 3.1 %slice.8 = f32[64,8192]{1,0:T(8,128)} slice(f32[64,9216]{1,0:T(8,128)} %bitcast.29), slice={[0:64], [0:8192]} | slice | bytes 4194304 | tf_op jit(solution)/shard_map/slice | solution.py:102
  231.5 2.7 %reshape.48 = f32[2048,256]{1,0:T(8,128)} reshape(f32[64,8192]{1,0:T(8,128)} %slice.8) | data formatting | bytes 4194304 | tf_op jit(solution)/shard_map/reshape | solution.py:102
  234.3 7.3 %all-to-all-done.6 = f32[64,1,1024]{2,1,0:T(1,128)S(1)} async-done(((f32[64,1,1024]{2,1,0:T(1,128)}), f32[64,1,1024]{2,1,0:T(1,128)S(1)}, u32[]{:S(2)}, u32[]{:S(2)}) %all-to-all-start.6) | async-done | bytes 262176 | tf_op jit(solution)/shard_map/all_to_all | solution.py:14
  242.9 3.6 %fusion = f32[2048,256]{1,0:T(8,128)S(1)} fusion(f32[2048,256]{1,0:T(8,128)} %reshape.48, f32[2048,256]{1,0:T(8,128)S(1)} %fusion.4, f32[256,256]{1,0:T(8,128)S(1)} %reshape.49), kind=kOutput, calls=%fused_computation.3 | convolution fusion | flops 1611661312 | bytes 6553600 | tf_op jit(solution)/shard_map/dot_general | solution.py:10
  246.5 3.5 %convolution_subtract_fusion.1 = f32[256,2048]{1,0:T(8,128)S(1)} fusion(f32[256,2048]{1,0:T(8,128)S(1)} %copy-done.3, f32[256,256]{1,0:T(8,128)S(1)} %fusion.3, f32[2048,256]{1,0:T(8,128)S(1)} %fusion), kind=kOutput, calls=%fused_computation.1 | convolution fusion | flops 1611137024 | bytes 6553600 | tf_op jit(solution)/shard_map/dot_general | solution.py:10
  250.1 3.4 %convolution_subtract_fusion = f32[256,2048]{1,0:T(8,128)} fusion(f32[256,2048]{1,0:T(8,128)S(1)} %convolution_subtract_fusion.1, f32[256,256]{1,0:T(8,128)S(1)} %fusion.1, f32[2048,256]{1,0:T(8,128)S(1)} %fusion.4), kind=kOutput, calls=%fused_computation | convolution fusion | flops 1611137024 | bytes 6553600 | tf_op jit(solution)/shard_map/dot_general | solution.py:10
  (31 shorter events, 5.9 us)
Async XLA Ops:
  0.6 1.0 copy-start
  27.6 17.9 %all-to-all-start.1 = ((f32[64,4,256]{2,1,0:T(4,128)}), f32[64,4,256]{2,1,0:T(4,128)S(1)}, u32[]{:S(2)}, u32[]{:S(2)}) async-start(f32[64,4,256]{2,1,0:T(4,128)} %broadcast_in_dim.12), calls=%async_computation.1 | async-start | bytes 524288 | tf_op jit(solution)/shard_map/all_to_all | solution.py:14
  47.0 59.1 %all-to-all-start.2 = ((f32[64,32,256]{2,1,0:T(8,128)}), f32[64,32,256]{2,1,0:T(8,128)S(1)}, u32[]{:S(2)}, u32[]{:S(2)}) async-start(f32[64,32,256]{2,1,0:T(8,128)} %broadcast_in_dim.13), calls=%async_computation.2 | async-start | bytes 4194304 | tf_op jit(solution)/shard_map/all_to_all | solution.py:14
  106.1 1.3 copy-start.4
  107.4 3.6 %copy-start.2 = (f32[256,2048]{1,0:T(8,128)S(1)}, f32[256,2048]{1,0:T(8,128)}, u32[]{:S(2)}) copy-start(f32[256,2048]{1,0:T(8,128)} %param.3) | copy-start | bytes 6291460
  111.0 26.8 %copy-start.5 = (f32[256,256]{1,0:T(8,128)S(1)}, f32[256,256]{1,0:T(8,128)}, u32[]{:S(2)}) copy-start(f32[256,256]{1,0:T(8,128)} %shard_map.41) | copy-start | bytes 786436
  134.4 12.5 %all-to-all-start.4 = ((f32[8,32,256]{2,1,0:T(8,128)}), f32[8,32,256]{2,1,0:T(8,128)S(1)}, u32[]{:S(2)}, u32[]{:S(2)}) async-start(f32[8,32,256]{2,1,0:T(8,128)} %broadcast_in_dim.16), calls=%async_computation.4 | async-start | bytes 524288 | tf_op jit(solution)/shard_map/all_to_all | solution.py:14
  221.6 1.4 copy-start.1
  223.9 17.6 %all-to-all-start.6 = ((f32[64,1,1024]{2,1,0:T(1,128)}), f32[64,1,1024]{2,1,0:T(1,128)S(1)}, u32[]{:S(2)}, u32[]{:S(2)}) async-start(f32[64,1,1024]{2,1,0:T(1,128)} %broadcast_in_dim.17), calls=%async_computation.6 | async-start | bytes 524288 | tf_op jit(solution)/shard_map/all_to_all | solution.py:14
  242.2 4.3 %copy-start.6 = (f32[256,256]{1,0:T(8,128)}, f32[256,256]{1,0:T(8,128)S(1)}, u32[]{:S(2)}) copy-start(f32[256,256]{1,0:T(8,128)S(1)} %reshape.49) | copy-start | bytes 786436
  242.9 3.7 %copy-start.3 = (f32[256,2048]{1,0:T(8,128)S(1)}, f32[256,2048]{1,0:T(8,128)}, u32[]{:S(2)}) copy-start(f32[256,2048]{1,0:T(8,128)} %param.3) | copy-start | bytes 6291460

commit v8 on v7

--- a/solution.py
+++ b/solution.py
@@ -20,38 +20,51 @@
     cols = lax.broadcasted_iota(jnp.int32, (n, n), 1)
     a_ref[...] = g_ref[...]
     w_ref[...] = jnp.where(rows == cols, 1.0, 0.0).astype(w_ref.dtype)
-    lane = lax.broadcasted_iota(jnp.int32, (8, n), 1)
     sub = lax.broadcasted_iota(jnp.int32, (8, 1), 0)
 
-    def block(b, carry):
+    def block(b, lo, wc):
         k0 = pl.multiple_of(b * 8, 8)
-        r = a_ref[pl.ds(k0, 8), :]
-        wb = w_ref[pl.ds(k0, 8), :]
+        lane = lax.broadcasted_iota(jnp.int32, (8, n - lo), 1) + lo
+        r = a_ref[pl.ds(k0, 8), lo:]
+        wb = w_ref[pl.ds(k0, 8), :wc]
         scale = jnp.zeros((8, 1), r.dtype)
         for s in range(8):
             k = k0 + s
             row = r[s : s + 1, :]
-            piv = jnp.sum(jnp.where(lane[0:1] == k, row, 0.0))
             col = jnp.sum(jnp.where(lane == k, r, 0.0), axis=1, keepdims=True)
+            piv = col[s : s + 1, :]
             fb = jnp.where(sub > s, col / piv, 0.0)
             r = r - fb * row
             wb = wb - fb * wb[s : s + 1, :]
             scale = jnp.where(sub == s, 1.0 / piv, scale)
         f = jnp.where(lane >= k0 + 8, r * scale, 0.0).T
-        a_ref[pl.ds(k0, 8), :] = r
-        w_ref[pl.ds(k0, 8), :] = wb
-        for c0 in range(0, n, 32):
-            fc = f[c0 : c0 + 32, :]
-            upd_a = a_ref[c0 : c0 + 32, :]
-            upd_w = w_ref[c0 : c0 + 32, :]
-            for s in range(8):
-                upd_a = upd_a - fc[:, s : s + 1] * r[s : s + 1, :]
-                upd_w = upd_w - fc[:, s : s + 1] * wb[s : s + 1, :]
-            a_ref[c0 : c0 + 32, :] = upd_a
-            w_ref[c0 : c0 + 32, :] = upd_w
+        a_ref[pl.ds(k0, 8), lo:] = r
+        w_ref[pl.ds(k0, 8), :wc] = wb
+        for c0 in range(lo, n, 32):
+
+            @pl.when(c0 + 32 > k0 + 8)
+            def _():
+                fc = f[c0 - lo : c0 - lo + 32, :]
+                upd_a = a_ref[c0 : c0 + 32, lo:]
+                upd_w = w_ref[c0 : c0 + 32, :wc]
+                for s in range(8):
+                    upd_a = upd_a - fc[:, s : s + 1] * r[s : s + 1, :]
+                    upd_w = upd_w - fc[:, s : s + 1] * wb[s : s + 1, :]
+                a_ref[c0 : c0 + 32, lo:] = upd_a
+                w_ref[c0 : c0 + 32, :wc] = upd_w
+
+    h = n // 2
+
+    def first(b, carry):
+        block(b, 0, h)
         return carry
 
-    lax.fori_loop(0, n // 8, block, 0)
+    def second(b, carry):
+        block(b, h, n)
+        return carry
+
+    lax.fori_loop(0, h // 8, first, 0)
+    lax.fori_loop(h // 8, n // 8, second, 0)
     diag = jnp.sum(jnp.where(rows == cols, a_ref[...], 0.0), axis=1, keepdims=True)
     w_ref[...] = w_ref[...] / jnp.sqrt(diag)
 

time: 254 us -> 247 us (0.972)
  Pallas kernels: 53.5 us -> 42.6 us
  waiting for transfers between devices: 29 us -> 35.4 us
  blocking collectives: 117 us -> 114 us
    pallas_call x1, Pallas kernels: 53.5 us -> 42.6 us  [_inverse_cholesky(): pl.pallas_call(_inverse_cholesky_kernel, out_shape=jax.ShapeDtypeStruct((...]
    all_to_all x4, waiting for transfers between devices: 29 us -> 35.4 us  [_exchange(): return lax.all_to_all(x, axis, 0, 0, tiled=False)]
    all_to_all x3, blocking collectives: 117 us -> 114 us  [_exchange(): return lax.all_to_all(x, axis, 0, 0, tiled=False)]
  transfers between devices with their start and end apart: 4 -> 4, of which waited for: 3 -> 4; matrix products, arithmetic and copies ran while one was open for 3% -> 3% of each run, Pallas kernels for 21% -> 17%
where the time goes in v8:
time: 247 us; the launch traced here: 246 us
  blocking collectives  114 us (46%)
  Pallas kernels  42.6 us (17%)
  waiting for transfers between devices  35.4 us (14%)
  matrix products  18.1 us (7%)
  starting transfers between devices  17.7 us (7%)
  local copies, waits for them, and re-layouts  16.4 us (7%)
    all_to_all x3, blocking collectives, _exchange(): return lax.all_to_all(x, axis, 0, 0, tiled=False)  114 us
    pallas_call x1, Pallas kernels, _inverse_cholesky(): pl.pallas_call(_inverse_cholesky_kernel, out_shape=jax.ShapeDtypeStruct((...  42.6 us
    all_to_all x4, waiting for transfers between devices, _exchange(): return lax.all_to_all(x, axis, 0, 0, tiled=False)  35.4 us
    dot_general x9, matrix products, _dot(): return jnp.dot(a, b, precision=lax.Precision.HIGHEST)  18.1 us
    all_to_all x4, starting transfers between devices, _exchange(): return lax.all_to_all(x, axis, 0, 0, tiled=False)  17.7 us
  transfers between devices with their start and end apart: 4, of which 4 were waited for; matrix products, arithmetic and copies ran while one was open for 3% of the time, Pallas kernels for 17%

profile of v8, /device:TPU:1, one launch (start us, length us, event | category | flops | bytes accessed | tf_op | source)
XLA Modules:
  0.0 246.1 jit_solution(2879297681705535025)
XLA Ops:
  0.6 0.9 copy-done
  2.3 24.5 %all_to_all.43 = f32[64,4,256]{2,1,0:T(4,128)S(1)} all-to-all(f32[64,4,256]{2,1,0:T(4,128)S(1)} %reshape.42), channel_id=1, replica_groups=mesh['row'=64,'col'=8] {'row'}, dimensions={0} | all-to-all | bytes 524288 | tf_op jit(solution)/shard_map/all_to_all | solution.py:14
  27.6 4.8 %all-to-all-start.1 = ((f32[64,4,256]{2,1,0:T(4,128)}), f32[64,4,256]{2,1,0:T(4,128)S(1)}, u32[]{:S(2)}, u32[]{:S(2)}) async-start(f32[64,4,256]{2,1,0:T(4,128)} %broadcast_in_dim.12), calls=%async_computation.1 | async-start | bytes 524288 | tf_op jit(solution)/shard_map/all_to_all | solution.py:14
  32.4 13.1 %all-to-all-done.1 = f32[64,4,256]{2,1,0:T(4,128)S(1)} async-done(((f32[64,4,256]{2,1,0:T(4,128)}), f32[64,4,256]{2,1,0:T(4,128)S(1)}, u32[]{:S(2)}, u32[]{:S(2)}) %all-to-all-start.1) | async-done | bytes 262176 | tf_op jit(solution)/shard_map/all_to_all | solution.py:14
  45.4 1.6 broadcast_in_dim.13
  47.0 4.8 %all-to-all-start.2 = ((f32[64,32,256]{2,1,0:T(8,128)}), f32[64,32,256]{2,1,0:T(8,128)S(1)}, u32[]{:S(2)}, u32[]{:S(2)}) async-start(f32[64,32,256]{2,1,0:T(8,128)} %broadcast_in_dim.13), calls=%async_computation.2 | async-start | bytes 4194304 | tf_op jit(solution)/shard_map/all_to_all | solution.py:14
  52.6 42.6 %shard_map.41 = f32[256,256]{1,0:T(8,128)} custom-call(f32[256,256]{1,0:T(8,128)} %reshape.43.g_ref), custom_call_target="tpu_custom_call" | custom-call | flops 33554432 | bytes 524288 | tf_op jit(solution)/shard_map/pallas_call | solution.py:74
  95.1 6.4 %all-to-all-done.2 = f32[64,32,256]{2,1,0:T(8,128)S(1)} async-done(((f32[64,32,256]{2,1,0:T(8,128)}), f32[64,32,256]{2,1,0:T(8,128)S(1)}, u32[]{:S(2)}, u32[]{:S(2)}) %all-to-all-start.2) | async-done | bytes 2097184 | tf_op jit(solution)/shard_map/all_to_all | solution.py:14
  101.5 1.3 copy-done.4
  102.8 3.6 %fusion.4 = f32[2048,256]{1,0:T(8,128)S(1)} fusion(f32[2048,256]{1,0:T(8,128)} %bitcast.30, f32[256,256]{1,0:T(8,128)} %shard_map.41), kind=kOutput, calls=%fused_computation.12 | convolution fusion | flops 1610612736 | bytes 4456448 | tf_op jit(solution)/shard_map/dot_general | solution.py:10
  106.4 2.0 fusion.5
  108.4 19.3 %all_to_all.44 = f32[8,32,256]{2,1,0:T(8,128)S(1)} all-to-all(f32[8,32,256]{2,1,0:T(8,128)S(1)} %bitcast.33), channel_id=1, replica_groups=mesh['row'=64,'col'=8] {'col'}, dimensions={0} | all-to-all | bytes 524288 | tf_op jit(solution)/shard_map/all_to_all | solution.py:14
  128.5 3.6 %all-to-all-start.4 = ((f32[8,32,256]{2,1,0:T(8,128)}), f32[8,32,256]{2,1,0:T(8,128)S(1)}, u32[]{:S(2)}, u32[]{:S(2)}) async-start(f32[8,32,256]{2,1,0:T(8,128)} %broadcast_in_dim.16), calls=%async_computation.4 | async-start | bytes 524288 | tf_op jit(solution)/shard_map/all_to_all | solution.py:14
  132.5 8.7 %all-to-all-done.4 = f32[8,32,256]{2,1,0:T(8,128)S(1)} async-done(((f32[8,32,256]{2,1,0:T(8,128)}), f32[8,32,256]{2,1,0:T(8,128)S(1)}, u32[]{:S(2)}, u32[]{:S(2)}) %all-to-all-start.4) | async-done | bytes 262176 | tf_op jit(solution)/shard_map/all_to_all | solution.py:14
  141.9 1.6 all_to_all.32
  143.5 70.3 %all_to_all.45 = f32[64,1,9216]{2,1,0:T(1,128)S(1)} all-to-all(f32[64,1,9216]{2,1,0:T(1,128)S(1)} %all_to_all.32), channel_id=1, replica_groups=mesh['row'=64,'col'=8] {'row'}, dimensions={0} | all-to-all | bytes 4718592 | tf_op jit(solution)/shard_map/all_to_all | solution.py:14
  214.3 1.4 copy-done.1
  216.5 4.5 %all-to-all-start.6 = ((f32[64,1,1024]{2,1,0:T(1,128)}), f32[64,1,1024]{2,1,0:T(1,128)S(1)}, u32[]{:S(2)}, u32[]{:S(2)}) async-start(f32[64,1,1024]{2,1,0:T(1,128)} %broadcast_in_dim.17), calls=%async_computation.6 | async-start | bytes 524288 | tf_op jit(solution)/shard_map/all_to_all | solution.py:14
  221.1 3.1 %slice.8 = f32[64,8192]{1,0:T(8,128)} slice(f32[64,9216]{1,0:T(8,128)} %bitcast.29), slice={[0:64], [0:8192]} | slice | bytes 4194304 | tf_op jit(solution)/shard_map/slice | solution.py:115
  224.2 2.7 %reshape.48 = f32[2048,256]{1,0:T(8,128)} reshape(f32[64,8192]{1,0:T(8,128)} %slice.8) | data formatting | bytes 4194304 | tf_op jit(solution)/shard_map/reshape | solution.py:115
  226.9 7.3 %all-to-all-done.6 = f32[64,1,1024]{2,1,0:T(1,128)S(1)} async-done(((f32[64,1,1024]{2,1,0:T(1,128)}), f32[64,1,1024]{2,1,0:T(1,128)S(1)}, u32[]{:S(2)}, u32[]{:S(2)}) %all-to-all-start.6) | async-done | bytes 262176 | tf_op jit(solution)/shard_map/all_to_all | solution.py:14
  235.5 3.6 %fusion = f32[2048,256]{1,0:T(8,128)S(1)} fusion(f32[2048,256]{1,0:T(8,128)} %reshape.48, f32[2048,256]{1,0:T(8,128)S(1)} %fusion.4, f32[256,256]{1,0:T(8,128)S(1)} %reshape.49), kind=kOutput, calls=%fused_computation.3 | convolution fusion | flops 1611661312 | bytes 6553600 | tf_op jit(solution)/shard_map/dot_general | solution.py:10
  239.1 3.5 %convolution_subtract_fusion.1 = f32[256,2048]{1,0:T(8,128)S(1)} fusion(f32[256,2048]{1,0:T(8,128)S(1)} %copy-done.3, f32[256,256]{1,0:T(8,128)S(1)} %fusion.3, f32[2048,256]{1,0:T(8,128)S(1)} %fusion), kind=kOutput, calls=%fused_computation.1 | convolution fusion | flops 1611137024 | bytes 6553600 | tf_op jit(solution)/shard_map/dot_general | solution.py:10
  242.7 3.4 %convolution_subtract_fusion = f32[256,2048]{1,0:T(8,128)} fusion(f32[256,2048]{1,0:T(8,128)S(1)} %convolution_subtract_fusion.1, f32[256,256]{1,0:T(8,128)S(1)} %fusion.1, f32[2048,256]{1,0:T(8,128)S(1)} %fusion.4), kind=kOutput, calls=%fused_computation | convolution fusion | flops 1611137024 | bytes 6553600 | tf_op jit(solution)/shard_map/dot_general | solution.py:10
  (31 shorter events, 6.7 us)
Async XLA Ops:
  0.6 1.0 copy-start
  27.6 17.9 %all-to-all-start.1 = ((f32[64,4,256]{2,1,0:T(4,128)}), f32[64,4,256]{2,1,0:T(4,128)S(1)}, u32[]{:S(2)}, u32[]{:S(2)}) async-start(f32[64,4,256]{2,1,0:T(4,128)} %broadcast_in_dim.12), calls=%async_computation.1 | async-start | bytes 524288 | tf_op jit(solution)/shard_map/all_to_all | solution.py:14
  47.0 54.5 %all-to-all-start.2 = ((f32[64,32,256]{2,1,0:T(8,128)}), f32[64,32,256]{2,1,0:T(8,128)S(1)}, u32[]{:S(2)}, u32[]{:S(2)}) async-start(f32[64,32,256]{2,1,0:T(8,128)} %broadcast_in_dim.13), calls=%async_computation.2 | async-start | bytes 4194304 | tf_op jit(solution)/shard_map/all_to_all | solution.py:14
  101.5 1.3 copy-start.4
  102.8 3.6 %copy-start.2 = (f32[256,2048]{1,0:T(8,128)S(1)}, f32[256,2048]{1,0:T(8,128)}, u32[]{:S(2)}) copy-start(f32[256,2048]{1,0:T(8,128)} %param.3) | copy-start | bytes 6291460
  106.4 25.6 %copy-start.5 = (f32[256,256]{1,0:T(8,128)S(1)}, f32[256,256]{1,0:T(8,128)}, u32[]{:S(2)}) copy-start(f32[256,256]{1,0:T(8,128)} %shard_map.41) | copy-start | bytes 786436
  128.5 12.8 %all-to-all-start.4 = ((f32[8,32,256]{2,1,0:T(8,128)}), f32[8,32,256]{2,1,0:T(8,128)S(1)}, u32[]{:S(2)}, u32[]{:S(2)}) async-start(f32[8,32,256]{2,1,0:T(8,128)} %broadcast_in_dim.16), calls=%async_computation.4 | async-start | bytes 524288 | tf_op jit(solution)/shard_map/all_to_all | solution.py:14
  214.2 1.4 copy-start.1
  216.5 17.6 %all-to-all-start.6 = ((f32[64,1,1024]{2,1,0:T(1,128)}), f32[64,1,1024]{2,1,0:T(1,128)S(1)}, u32[]{:S(2)}, u32[]{:S(2)}) async-start(f32[64,1,1024]{2,1,0:T(1,128)} %broadcast_in_dim.17), calls=%async_computation.6 | async-start | bytes 524288 | tf_op jit(solution)/shard_map/all_to_all | solution.py:14
  234.9 4.3 %copy-start.6 = (f32[256,256]{1,0:T(8,128)}, f32[256,256]{1,0:T(8,128)S(1)}, u32[]{:S(2)}) copy-start(f32[256,256]{1,0:T(8,128)S(1)} %reshape.49) | copy-start | bytes 786436
  235.5 3.7 %copy-start.3 = (f32[256,2048]{1,0:T(8,128)S(1)}, f32[256,2048]{1,0:T(8,128)}, u32[]{:S(2)}) copy-start(f32[256,2048]{1,0:T(8,128)} %param.3) | copy-start | bytes 6291460

commit v9 on v8

--- a/solution.py
+++ b/solution.py
@@ -116,10 +116,11 @@
     band_rows = got[:, piece * k :].sum(0)
     band_block = _exchange(jnp.broadcast_to(band_rows[None], (n_row,) + band_rows.shape), "row").reshape(k, k)
 
-    corrected_own = moment_own - 0.5 * _dot(basis_own, band_block)
-    corrected_stored = moment_stored - 0.5 * _dot(basis_stored, band_block)
-    updated = affinity - _dot(basis_own, corrected_stored.T)
-    updated = updated - _dot(corrected_own, basis_stored.T)
+    left = jnp.concatenate([basis_own, moment_own], axis=1)
+    right = jnp.concatenate([moment_stored, basis_stored], axis=1)
+    updated = affinity - _dot(left, right.T)
+    sym_band = 0.5 * (band_block + band_block.T)
+    updated = updated + _dot(_dot(basis_own, sym_band), basis_stored.T)
     return (updated, band_block)
 
 

time: 247 us -> 245 us (level)
  waiting for transfers between devices: 35.4 us -> 28.1 us
  local copies, waits for them, and re-layouts: 16.4 us -> 19.6 us
    all_to_all x4, waiting for transfers between devices: 35.4 us -> 28.1 us  [_exchange(): return lax.all_to_all(x, axis, 0, 0, tiled=False)]
    reshape x1 -> x2, local copies, waits for them, and re-layouts: 2.72 us -> 5.6 us  [shards(): moment_stored = got[:, :piece * k].reshape(n_row * piece, k)]
    dot_general x9 -> x8, matrix products: 18.1 us -> 20.1 us  [_dot(): return jnp.dot(a, b, precision=lax.Precision.HIGHEST)]
  transfers between devices with their start and end apart: 4 -> 4, of which waited for: 4 -> 3; matrix products, arithmetic and copies ran while one was open for 3% -> 7% of each run, Pallas kernels for 17% -> 17%
where the time goes in v9:
time: 245 us; the launch traced here: 244 us
  blocking collectives  114 us (47%)
  Pallas kernels  42.6 us (17%)
  waiting for transfers between devices  28.1 us (11%)
  matrix products  20.1 us (8%)
  local copies, waits for them, and re-layouts  19.6 us (8%)
  starting transfers between devices  17.7 us (7%)
    all_to_all x3, blocking collectives, _exchange(): return lax.all_to_all(x, axis, 0, 0, tiled=False)  114 us
    pallas_call x1, Pallas kernels, _inverse_cholesky(): pl.pallas_call(_inverse_cholesky_kernel, out_shape=jax.ShapeDtypeStruct((...  42.6 us
    all_to_all x4, waiting for transfers between devices, _exchange(): return lax.all_to_all(x, axis, 0, 0, tiled=False)  28.1 us
    dot_general x8, matrix products, _dot(): return jnp.dot(a, b, precision=lax.Precision.HIGHEST)  20.1 us
    all_to_all x4, starting transfers between devices, _exchange(): return lax.all_to_all(x, axis, 0, 0, tiled=False)  17.7 us
    reshape x2, local copies, waits for them, and re-layouts, shards(): moment_stored = got[:, :piece * k].reshape(n_row * piece, k)  5.6 us
  transfers between devices with their start and end apart: 4, of which 3 were waited for; matrix products, arithmetic and copies ran while one was open for 7% of the time, Pallas kernels for 17%

profile of v9, /device:TPU:1, one launch (start us, length us, event | category | flops | bytes accessed | tf_op | source)
XLA Modules:
  0.0 243.9 jit_solution(11819764929464054761)
XLA Ops:
  0.6 0.9 copy-done
  2.3 24.5 %all_to_all.43 = f32[64,4,256]{2,1,0:T(4,128)S(1)} all-to-all(f32[64,4,256]{2,1,0:T(4,128)S(1)} %reshape.42), channel_id=1, replica_groups=mesh['row'=64,'col'=8] {'row'}, dimensions={0} | all-to-all | bytes 524288 | tf_op jit(solution)/shard_map/all_to_all | solution.py:14
  27.6 4.8 %all-to-all-start.1 = ((f32[64,4,256]{2,1,0:T(4,128)}), f32[64,4,256]{2,1,0:T(4,128)S(1)}, u32[]{:S(2)}, u32[]{:S(2)}) async-start(f32[64,4,256]{2,1,0:T(4,128)} %broadcast_in_dim.12), calls=%async_computation.1 | async-start | bytes 524288 | tf_op jit(solution)/shard_map/all_to_all | solution.py:14
  32.4 13.1 %all-to-all-done.1 = f32[64,4,256]{2,1,0:T(4,128)S(1)} async-done(((f32[64,4,256]{2,1,0:T(4,128)}), f32[64,4,256]{2,1,0:T(4,128)S(1)}, u32[]{:S(2)}, u32[]{:S(2)}) %all-to-all-start.1) | async-done | bytes 262176 | tf_op jit(solution)/shard_map/all_to_all | solution.py:14
  45.4 1.6 broadcast_in_dim.13
  47.0 4.8 %all-to-all-start.2 = ((f32[64,32,256]{2,1,0:T(8,128)}), f32[64,32,256]{2,1,0:T(8,128)S(1)}, u32[]{:S(2)}, u32[]{:S(2)}) async-start(f32[64,32,256]{2,1,0:T(8,128)} %broadcast_in_dim.13), calls=%async_computation.2 | async-start | bytes 4194304 | tf_op jit(solution)/shard_map/all_to_all | solution.py:14
  52.6 42.6 %shard_map.41 = f32[256,256]{1,0:T(8,128)} custom-call(f32[256,256]{1,0:T(8,128)} %reshape.43.g_ref), custom_call_target="tpu_custom_call" | custom-call | flops 33554432 | bytes 524288 | tf_op jit(solution)/shard_map/pallas_call | solution.py:74
  95.1 6.4 %all-to-all-done.2 = f32[64,32,256]{2,1,0:T(8,128)S(1)} async-done(((f32[64,32,256]{2,1,0:T(8,128)}), f32[64,32,256]{2,1,0:T(8,128)S(1)}, u32[]{:S(2)}, u32[]{:S(2)}) %all-to-all-start.2) | async-done | bytes 2097184 | tf_op jit(solution)/shard_map/all_to_all | solution.py:14
  101.5 1.3 copy-done.3
  102.8 3.7 %fusion.18 = f32[2048,256]{0,1:T(8,128)S(1)} fusion(f32[2048,256]{1,0:T(8,128)} %bitcast.31, f32[256,256]{1,0:T(8,128)} %shard_map.41), kind=kOutput, calls=%fused_computation.21 | convolution fusion | flops 1610612736 | bytes 4456448 | tf_op jit(solution)/shard_map/dot_general | solution.py:10
  106.6 1.9 fusion.19
  108.5 19.3 %all_to_all.44 = f32[8,32,256]{2,1,0:T(8,128)S(1)} all-to-all(f32[8,32,256]{2,1,0:T(8,128)S(1)} %bitcast.35), channel_id=1, replica_groups=mesh['row'=64,'col'=8] {'col'}, dimensions={0} | all-to-all | bytes 524288 | tf_op jit(solution)/shard_map/all_to_all | solution.py:14
  128.5 3.6 %all-to-all-start.4 = ((f32[8,32,256]{2,1,0:T(8,128)}), f32[8,32,256]{2,1,0:T(8,128)S(1)}, u32[]{:S(2)}, u32[]{:S(2)}) async-start(f32[8,32,256]{2,1,0:T(8,128)} %broadcast_in_dim.14), calls=%async_computation.4 | async-start | bytes 524288 | tf_op jit(solution)/shard_map/all_to_all | solution.py:14
  132.5 8.7 %all-to-all-done.4 = f32[8,32,256]{2,1,0:T(8,128)S(1)} async-done(((f32[8,32,256]{2,1,0:T(8,128)}), f32[8,32,256]{2,1,0:T(8,128)S(1)}, u32[]{:S(2)}, u32[]{:S(2)}) %all-to-all-start.4) | async-done | bytes 262176 | tf_op jit(solution)/shard_map/all_to_all | solution.py:14
  141.9 1.6 all_to_all.32
  143.5 70.3 %all_to_all.45 = f32[64,1,9216]{2,1,0:T(1,128)S(1)} all-to-all(f32[64,1,9216]{2,1,0:T(1,128)S(1)} %all_to_all.32), channel_id=1, replica_groups=mesh['row'=64,'col'=8] {'row'}, dimensions={0} | all-to-all | bytes 4718592 | tf_op jit(solution)/shard_map/all_to_all | solution.py:14
  214.3 1.4 copy-done.1
  215.7 0.8 broadcast_in_dim.17
  216.5 4.5 %all-to-all-start.6 = ((f32[64,1,1024]{2,1,0:T(1,128)}), f32[64,1,1024]{2,1,0:T(1,128)S(1)}, u32[]{:S(2)}, u32[]{:S(2)}) async-start(f32[64,1,1024]{2,1,0:T(1,128)} %broadcast_in_dim.17), calls=%async_computation.6 | async-start | bytes 524288 | tf_op jit(solution)/shard_map/all_to_all | solution.py:14
  221.2 3.1 %slice.8 = f32[64,8192]{1,0:T(8,128)} slice(f32[64,9216]{1,0:T(8,128)} %bitcast.30), slice={[0:64], [0:8192]} | slice | bytes 4194304 | tf_op jit(solution)/shard_map/slice | solution.py:115
  224.3 2.7 %reshape.48 = f32[2048,256]{1,0:T(8,128)} reshape(f32[64,8192]{1,0:T(8,128)} %slice.8) | data formatting | bytes 4194304 | tf_op jit(solution)/shard_map/reshape | solution.py:115
  227.0 2.9 %copy.9 = f32[2048,256]{0,1:T(8,128)} copy(f32[2048,256]{1,0:T(8,128)} %reshape.48) | data formatting | bytes 4194304 | tf_op jit(solution)/shard_map/reshape | solution.py:115
  229.9 7.7 %fusion.4 = f32[256,2048]{1,0:T(8,128)} fusion(f32[256,2048]{1,0:T(8,128)} %param.3, f32[2048,256]{0,1:T(8,128)S(1)} %fusion.18, f32[2048,256]{0,1:T(8,128)} %copy.9, f32[256,256]{0,1:T(8,128)S(1)} %copy.8, f32[256,256]{0,1:T(8,128)S(1)} %bitcast.32), kind=kOutput, calls=%fused_computation.4 | convolution fusion | flops 3222929408 | bytes 8912896 | tf_op jit(solution)/shard_map/dot_general | solution.py:10
  239.0 4.8 %convolution_add_fusion = f32[256,2048]{1,0:T(8,128)} fusion(f32[256,2048]{1,0:T(8,128)} %fusion.4, f32[256,256]{1,0:T(8,128)S(1)} %fusion.11, f32[2048,256]{0,1:T(8,128)S(1)} %fusion.18), kind=kOutput, calls=%fused_computation.5 | convolution fusion | flops 1611137024 | bytes 6553600 | tf_op jit(solution)/shard_map/dot_general | solution.py:10
  (31 shorter events, 6.1 us)
Async XLA Ops:
  0.6 1.0 copy-start
  27.6 17.9 %all-to-all-start.1 = ((f32[64,4,256]{2,1,0:T(4,128)}), f32[64,4,256]{2,1,0:T(4,128)S(1)}, u32[]{:S(2)}, u32[]{:S(2)}) async-start(f32[64,4,256]{2,1,0:T(4,128)} %broadcast_in_dim.12), calls=%async_computation.1 | async-start | bytes 524288 | tf_op jit(solution)/shard_map/all_to_all | solution.py:14
  47.0 54.5 %all-to-all-start.2 = ((f32[64,32,256]{2,1,0:T(8,128)}), f32[64,32,256]{2,1,0:T(8,128)S(1)}, u32[]{:S(2)}, u32[]{:S(2)}) async-start(f32[64,32,256]{2,1,0:T(8,128)} %broadcast_in_dim.13), calls=%async_computation.2 | async-start | bytes 4194304 | tf_op jit(solution)/shard_map/all_to_all | solution.py:14
  101.5 1.3 copy-start.3
  102.8 3.7 %copy-start.2 = (f32[256,2048]{1,0:T(8,128)S(1)}, f32[256,2048]{1,0:T(8,128)}, u32[]{:S(2)}) copy-start(f32[256,2048]{1,0:T(8,128)} %param.3) | copy-start | bytes 6291460
  106.6 25.5 %copy-start.4 = (f32[256,256]{1,0:T(8,128)S(1)}, f32[256,256]{1,0:T(8,128)}, u32[]{:S(2)}) copy-start(f32[256,256]{1,0:T(8,128)} %shard_map.41) | copy-start | bytes 786436
  128.5 12.8 %all-to-all-start.4 = ((f32[8,32,256]{2,1,0:T(8,128)}), f32[8,32,256]{2,1,0:T(8,128)S(1)}, u32[]{:S(2)}, u32[]{:S(2)}) async-start(f32[8,32,256]{2,1,0:T(8,128)} %broadcast_in_dim.14), calls=%async_computation.4 | async-start | bytes 524288 | tf_op jit(solution)/shard_map/all_to_all | solution.py:14
  214.3 1.4 copy-start.1
  216.5 21.0 %all-to-all-start.6 = ((f32[64,1,1024]{2,1,0:T(1,128)}), f32[64,1,1024]{2,1,0:T(1,128)S(1)}, u32[]{:S(2)}, u32[]{:S(2)}) async-start(f32[64,1,1024]{2,1,0:T(1,128)} %broadcast_in_dim.17), calls=%async_computation.6 | async-start | bytes 524288 | tf_op jit(solution)/shard_map/all_to_all | solution.py:14
  238.3 5.6 %copy-start.5 = (f32[256,256]{1,0:T(8,128)}, f32[256,256]{1,0:T(8,128)S(1)}, u32[]{:S(2)}) copy-start(f32[256,256]{1,0:T(8,128)S(1)} %reshape.49) | copy-start | bytes 786436

commit v10 on v9

--- a/solution.py
+++ b/solution.py
@@ -104,16 +104,18 @@
     moment_own = _exchange(jnp.broadcast_to(own_moment[None], (n_col, piece, k)), "col").reshape(local_rows, k)
     band_part = _dot(basis_own.T, moment_own)
 
+    lanes = 128
+    m_rows = piece * k // lanes
     send = jnp.concatenate(
         [
-            jnp.broadcast_to(own_moment.reshape(1, piece * k), (n_row, piece * k)),
-            band_part.reshape(n_row, (k // n_row) * k),
+            jnp.broadcast_to(own_moment.reshape(1, m_rows, lanes), (n_row, m_rows, lanes)),
+            band_part.reshape(n_row, (k // n_row) * k // lanes, lanes),
         ],
         axis=1,
     )
     got = _exchange(send, "row")
-    moment_stored = got[:, : piece * k].reshape(n_row * piece, k)
-    band_rows = got[:, piece * k :].sum(0)
+    moment_stored = got[:, :m_rows].reshape(n_row * piece, k)
+    band_rows = got[:, m_rows:].sum(0).reshape(k // n_row, k)
     band_block = _exchange(jnp.broadcast_to(band_rows[None], (n_row,) + band_rows.shape), "row").reshape(k, k)
 
     left = jnp.concatenate([basis_own, moment_own], axis=1)

time: 245 us -> 243 us (level)
  transfers between devices with their start and end apart: 4 -> 4, of which waited for: 3 -> 3; matrix products, arithmetic and copies ran while one was open for 7% -> 7% of each run, Pallas kernels for 17% -> 18%
where the time goes in v10:
time: 243 us; the launch traced here: 242 us
  blocking collectives  114 us (47%)
  Pallas kernels  42.6 us (18%)
  waiting for transfers between devices  28.3 us (12%)
  matrix products  20.1 us (8%)
  local copies, waits for them, and re-layouts  17.9 us (7%)
  starting transfers between devices  17.7 us (7%)
    all_to_all x3, blocking collectives, _exchange(): return lax.all_to_all(x, axis, 0, 0, tiled=False)  114 us
    pallas_call x1, Pallas kernels, _inverse_cholesky(): pl.pallas_call(_inverse_cholesky_kernel, out_shape=jax.ShapeDtypeStruct((...  42.6 us
    all_to_all x4, waiting for transfers between devices, _exchange(): return lax.all_to_all(x, axis, 0, 0, tiled=False)  28.3 us
    dot_general x8, matrix products, _dot(): return jnp.dot(a, b, precision=lax.Precision.HIGHEST)  20.1 us
    all_to_all x4, starting transfers between devices, _exchange(): return lax.all_to_all(x, axis, 0, 0, tiled=False)  17.7 us
    reshape x2, local copies, waits for them, and re-layouts, shards(): moment_stored = got[:, :m_rows].reshape(n_row * piece, k)  5.77 us
  transfers between devices with their start and end apart: 4, of which 3 were waited for; matrix products, arithmetic and copies ran while one was open for 7% of the time, Pallas kernels for 18%

profile of v10, /device:TPU:1, one launch (start us, length us, event | category | flops | bytes accessed | tf_op | source)
XLA Modules:
  0.0 241.9 jit_solution(8218281200778016334)
XLA Ops:
  0.6 0.9 copy-done
  2.3 24.5 %all_to_all.35 = f32[64,4,256]{2,1,0:T(4,128)S(1)} all-to-all(f32[64,4,256]{2,1,0:T(4,128)S(1)} %reshape.34), channel_id=1, replica_groups=mesh['row'=64,'col'=8] {'row'}, dimensions={0} | all-to-all | bytes 524288 | tf_op jit(solution)/shard_map/all_to_all | solution.py:14
  26.8 0.7 broadcast_in_dim.14
  27.6 4.8 %all-to-all-start.1 = ((f32[64,4,256]{2,1,0:T(4,128)}), f32[64,4,256]{2,1,0:T(4,128)S(1)}, u32[]{:S(2)}, u32[]{:S(2)}) async-start(f32[64,4,256]{2,1,0:T(4,128)} %broadcast_in_dim.14), calls=%async_computation.1 | async-start | bytes 524288 | tf_op jit(solution)/shard_map/all_to_all | solution.py:14
  32.4 13.1 %all-to-all-done.1 = f32[64,4,256]{2,1,0:T(4,128)S(1)} async-done(((f32[64,4,256]{2,1,0:T(4,128)}), f32[64,4,256]{2,1,0:T(4,128)S(1)}, u32[]{:S(2)}, u32[]{:S(2)}) %all-to-all-start.1) | async-done | bytes 262176 | tf_op jit(solution)/shard_map/all_to_all | solution.py:14
  45.4 1.6 broadcast_in_dim.15
  47.0 4.8 %all-to-all-start.2 = ((f32[64,32,256]{2,1,0:T(8,128)}), f32[64,32,256]{2,1,0:T(8,128)S(1)}, u32[]{:S(2)}, u32[]{:S(2)}) async-start(f32[64,32,256]{2,1,0:T(8,128)} %broadcast_in_dim.15), calls=%async_computation.2 | async-start | bytes 4194304 | tf_op jit(solution)/shard_map/all_to_all | solution.py:14
  51.8 0.8 reshape.35.g_ref
  52.6 42.6 %shard_map.41 = f32[256,256]{1,0:T(8,128)} custom-call(f32[256,256]{1,0:T(8,128)} %reshape.35.g_ref), custom_call_target="tpu_custom_call" | custom-call | flops 33554432 | bytes 524288 | tf_op jit(solution)/shard_map/pallas_call | solution.py:74
  95.2 6.3 %all-to-all-done.2 = f32[64,32,256]{2,1,0:T(8,128)S(1)} async-done(((f32[64,32,256]{2,1,0:T(8,128)}), f32[64,32,256]{2,1,0:T(8,128)S(1)}, u32[]{:S(2)}, u32[]{:S(2)}) %all-to-all-start.2) | async-done | bytes 2097184 | tf_op jit(solution)/shard_map/all_to_all | solution.py:14
  101.5 1.3 copy-done.3
  102.8 3.7 %fusion.18 = f32[2048,256]{0,1:T(8,128)S(1)} fusion(f32[2048,256]{1,0:T(8,128)} %bitcast.24, f32[256,256]{1,0:T(8,128)} %shard_map.41), kind=kOutput, calls=%fused_computation.20 | convolution fusion | flops 1610612736 | bytes 4456448 | tf_op jit(solution)/shard_map/dot_general | solution.py:10
  106.6 1.9 fusion.19
  108.5 19.3 %all_to_all.36 = f32[8,32,256]{2,1,0:T(8,128)S(1)} all-to-all(f32[8,32,256]{2,1,0:T(8,128)S(1)} %bitcast.28), channel_id=1, replica_groups=mesh['row'=64,'col'=8] {'col'}, dimensions={0} | all-to-all | bytes 524288 | tf_op jit(solution)/shard_map/all_to_all | solution.py:14
  128.5 3.4 %all-to-all-start.4 = ((f32[8,32,256]{2,1,0:T(8,128)}), f32[8,32,256]{2,1,0:T(8,128)S(1)}, u32[]{:S(2)}, u32[]{:S(2)}) async-start(f32[8,32,256]{2,1,0:T(8,128)} %broadcast_in_dim.16), calls=%async_computation.4 | async-start | bytes 524288 | tf_op jit(solution)/shard_map/all_to_all | solution.py:14
  132.3 8.9 %all-to-all-done.4 = f32[8,32,256]{2,1,0:T(8,128)S(1)} async-done(((f32[8,32,256]{2,1,0:T(8,128)}), f32[8,32,256]{2,1,0:T(8,128)S(1)}, u32[]{:S(2)}, u32[]{:S(2)}) %all-to-all-start.4) | async-done | bytes 262176 | tf_op jit(solution)/shard_map/all_to_all | solution.py:14
  142.1 70.3 %all_to_all.37 = f32[64,72,128]{2,1,0:T(8,128)S(1)} all-to-all(f32[64,72,128]{2,1,0:T(8,128)S(1)} %pad_maximum_fusion), channel_id=1, replica_groups=mesh['row'=64,'col'=8] {'row'}, dimensions={0} | all-to-all | bytes 4718592 | tf_op jit(solution)/shard_map/all_to_all | solution.py:14
  212.4 1.4 copy-done.1
  214.7 4.7 %all-to-all-start.6 = ((f32[64,4,256]{2,1,0:T(4,128)}), f32[64,4,256]{2,1,0:T(4,128)S(1)}, u32[]{:S(2)}, u32[]{:S(2)}) async-start(f32[64,4,256]{2,1,0:T(4,128)} %broadcast_in_dim.38), calls=%async_computation.6 | async-start | bytes 524288 | tf_op jit(solution)/shard_map/all_to_all | solution.py:14
  219.5 3.2 %slice.8 = f32[64,64,128]{2,1,0:T(8,128)} slice(f32[64,72,128]{2,1,0:T(8,128)} %copy-done.1), slice={[0:64], [0:64], [0:128]} | slice | bytes 4194304 | tf_op jit(solution)/shard_map/slice | solution.py:117
  222.7 2.9 %reshape.40 = f32[2048,256]{1,0:T(8,128)} reshape(f32[64,64,128]{2,1,0:T(8,128)} %slice.8) | data formatting | bytes 4194304 | tf_op jit(solution)/shard_map/reshape | solution.py:117
  225.6 2.9 %copy.6 = f32[2048,256]{0,1:T(8,128)} copy(f32[2048,256]{1,0:T(8,128)} %reshape.40) | data formatting | bytes 4194304 | tf_op jit(solution)/shard_map/reshape | solution.py:117
  228.5 7.7 %fusion.4 = f32[256,2048]{1,0:T(8,128)} fusion(f32[256,2048]{1,0:T(8,128)} %param.3, f32[2048,256]{0,1:T(8,128)S(1)} %fusion.18, f32[2048,256]{0,1:T(8,128)} %copy.6, f32[256,256]{0,1:T(8,128)S(1)} %copy.5, f32[256,256]{0,1:T(8,128)S(1)} %bitcast.25), kind=kOutput, calls=%fused_computation.4 | convolution fusion | flops 3222929408 | bytes 8912896 | tf_op jit(solution)/shard_map/dot_general | solution.py:10
  237.0 4.8 %convolution_add_fusion = f32[256,2048]{1,0:T(8,128)} fusion(f32[256,2048]{1,0:T(8,128)} %fusion.4, f32[256,256]{1,0:T(8,128)S(1)} %fusion.11, f32[2048,256]{0,1:T(8,128)S(1)} %fusion.18), kind=kOutput, calls=%fused_computation.5 | convolution fusion | flops 1611137024 | bytes 6553600 | tf_op jit(solution)/shard_map/dot_general | solution.py:10
  (29 shorter events, 4.6 us)
Async XLA Ops:
  0.6 1.0 copy-start
  27.6 17.9 %all-to-all-start.1 = ((f32[64,4,256]{2,1,0:T(4,128)}), f32[64,4,256]{2,1,0:T(4,128)S(1)}, u32[]{:S(2)}, u32[]{:S(2)}) async-start(f32[64,4,256]{2,1,0:T(4,128)} %broadcast_in_dim.14), calls=%async_computation.1 | async-start | bytes 524288 | tf_op jit(solution)/shard_map/all_to_all | solution.py:14
  47.0 54.5 %all-to-all-start.2 = ((f32[64,32,256]{2,1,0:T(8,128)}), f32[64,32,256]{2,1,0:T(8,128)S(1)}, u32[]{:S(2)}, u32[]{:S(2)}) async-start(f32[64,32,256]{2,1,0:T(8,128)} %broadcast_in_dim.15), calls=%async_computation.2 | async-start | bytes 4194304 | tf_op jit(solution)/shard_map/all_to_all | solution.py:14
  101.5 1.3 copy-start.3
  102.8 3.7 %copy-start.2 = (f32[256,2048]{1,0:T(8,128)S(1)}, f32[256,2048]{1,0:T(8,128)}, u32[]{:S(2)}) copy-start(f32[256,2048]{1,0:T(8,128)} %param.3) | copy-start | bytes 6291460
  106.6 25.3 %copy-start.4 = (f32[256,256]{1,0:T(8,128)S(1)}, f32[256,256]{1,0:T(8,128)}, u32[]{:S(2)}) copy-start(f32[256,256]{1,0:T(8,128)} %shard_map.41) | copy-start | bytes 786436
  128.5 12.8 %all-to-all-start.4 = ((f32[8,32,256]{2,1,0:T(8,128)}), f32[8,32,256]{2,1,0:T(8,128)S(1)}, u32[]{:S(2)}, u32[]{:S(2)}) async-start(f32[8,32,256]{2,1,0:T(8,128)} %broadcast_in_dim.16), calls=%async_computation.4 | async-start | bytes 524288 | tf_op jit(solution)/shard_map/all_to_all | solution.py:14
  212.4 1.4 copy-start.1
  214.7 21.5 %all-to-all-start.6 = ((f32[64,4,256]{2,1,0:T(4,128)}), f32[64,4,256]{2,1,0:T(4,128)S(1)}, u32[]{:S(2)}, u32[]{:S(2)}) async-start(f32[64,4,256]{2,1,0:T(4,128)} %broadcast_in_dim.38), calls=%async_computation.6 | async-start | bytes 524288 | tf_op jit(solution)/shard_map/all_to_all | solution.py:14
  236.3 5.6 %copy-start.5 = (f32[256,256]{1,0:T(8,128)}, f32[256,256]{1,0:T(8,128)S(1)}, u32[]{:S(2)}) copy-start(f32[256,256]{1,0:T(8,128)S(1)} %reshape.41) | copy-start | bytes 786436

commit v11 on v9

--- a/solution.py
+++ b/solution.py
@@ -104,21 +104,24 @@
     moment_own = _exchange(jnp.broadcast_to(own_moment[None], (n_col, piece, k)), "col").reshape(local_rows, k)
     band_part = _dot(basis_own.T, moment_own)
 
+    lanes = min(128, k)
+    parts = k // lanes
+    m_block = own_moment.reshape(piece, parts, lanes).transpose(1, 0, 2).reshape(parts * piece, lanes)
     send = jnp.concatenate(
         [
-            jnp.broadcast_to(own_moment.reshape(1, piece * k), (n_row, piece * k)),
-            band_part.reshape(n_row, (k // n_row) * k),
+            jnp.broadcast_to(m_block[None], (n_row, parts * piece, lanes)),
+            band_part.reshape(n_row, -1, lanes),
         ],
         axis=1,
     )
     got = _exchange(send, "row")
-    moment_stored = got[:, : piece * k].reshape(n_row * piece, k)
-    band_rows = got[:, piece * k :].sum(0)
+    moment_parts = [got[:, h * piece : (h + 1) * piece].reshape(n_row * piece, lanes) for h in range(parts)]
+    band_rows = got[:, parts * piece :].sum(0).reshape(k // n_row, k)
     band_block = _exchange(jnp.broadcast_to(band_rows[None], (n_row,) + band_rows.shape), "row").reshape(k, k)
 
-    left = jnp.concatenate([basis_own, moment_own], axis=1)
-    right = jnp.concatenate([moment_stored, basis_stored], axis=1)
-    updated = affinity - _dot(left, right.T)
+    updated = affinity - _dot(moment_own, basis_stored.T)
+    for h, part in enumerate(moment_parts):
+        updated = updated - _dot(basis_own[:, h * lanes : (h + 1) * lanes], part.T)
     sym_band = 0.5 * (band_block + band_block.T)
     updated = updated + _dot(_dot(basis_own, sym_band), basis_stored.T)
     return (updated, band_block)

time: 245 us -> 239 us (0.976)
  local copies, waits for them, and re-layouts: 19.6 us -> 10.6 us
  waiting for transfers between devices: 28.1 us -> 32.2 us
    reshape x4 -> x2, local copies, waits for them, and re-layouts: 5.8 us -> 0.04 us  [the longest x1 0.02 us: shards(): own_moment.reshape(piece, parts, lanes).transpose(1, 0, 2)]
    all_to_all x4, waiting for transfers between devices: 28.1 us -> 32.2 us  [_exchange(): return lax.all_to_all(x, axis, 0, 0, tiled=False)]
    dot_general x8 -> x10, matrix products: 20.1 us -> 19.8 us  [_dot(): return jnp.dot(a, b, precision=lax.Precision.HIGHEST)]
  transfers between devices with their start and end apart: 4 -> 4, of which waited for: 3 -> 4; matrix products, arithmetic and copies ran while one was open for 7% -> 4% of each run, Pallas kernels for 17% -> 18%
where the time goes in v11:
time: 239 us; the launch traced here: 238 us
  blocking collectives  114 us (48%)
  Pallas kernels  42.6 us (18%)
  waiting for transfers between devices  32.2 us (13%)
  matrix products  19.8 us (8%)
  starting transfers between devices  17.7 us (7%)
  local copies, waits for them, and re-layouts  10.6 us (4%)
    all_to_all x3, blocking collectives, _exchange(): return lax.all_to_all(x, axis, 0, 0, tiled=False)  114 us
    pallas_call x1, Pallas kernels, _inverse_cholesky(): pl.pallas_call(_inverse_cholesky_kernel, out_shape=jax.ShapeDtypeStruct((...  42.6 us
    all_to_all x4, waiting for transfers between devices, _exchange(): return lax.all_to_all(x, axis, 0, 0, tiled=False)  32.2 us
    dot_general x10, matrix products, _dot(): return jnp.dot(a, b, precision=lax.Precision.HIGHEST)  19.8 us
    all_to_all x4, starting transfers between devices, _exchange(): return lax.all_to_all(x, axis, 0, 0, tiled=False)  17.7 us
  transfers between devices with their start and end apart: 4, of which 4 were waited for; matrix products, arithmetic and copies ran while one was open for 4% of the time, Pallas kernels for 18%

profile of v11, /device:TPU:1, one launch (start us, length us, event | category | flops | bytes accessed | tf_op | source)
XLA Modules:
  0.0 238.2 jit_solution(10515104601728231244)
XLA Ops:
  0.6 0.9 copy-done
  2.3 24.5 %all_to_all.35 = f32[64,4,256]{2,1,0:T(4,128)S(1)} all-to-all(f32[64,4,256]{2,1,0:T(4,128)S(1)} %reshape.40), channel_id=1, replica_groups=mesh['row'=64,'col'=8] {'row'}, dimensions={0} | all-to-all | bytes 524288 | tf_op jit(solution)/shard_map/all_to_all | solution.py:14
  27.6 4.8 %all-to-all-start.2 = ((f32[64,4,256]{2,1,0:T(4,128)}), f32[64,4,256]{2,1,0:T(4,128)S(1)}, u32[]{:S(2)}, u32[]{:S(2)}) async-start(f32[64,4,256]{2,1,0:T(4,128)} %broadcast_in_dim.15), calls=%async_computation.2 | async-start | bytes 524288 | tf_op jit(solution)/shard_map/all_to_all | solution.py:14
  32.4 13.1 %all-to-all-done.2 = f32[64,4,256]{2,1,0:T(4,128)S(1)} async-done(((f32[64,4,256]{2,1,0:T(4,128)}), f32[64,4,256]{2,1,0:T(4,128)S(1)}, u32[]{:S(2)}, u32[]{:S(2)}) %all-to-all-start.2) | async-done | bytes 262176 | tf_op jit(solution)/shard_map/all_to_all | solution.py:14
  45.4 1.6 broadcast_in_dim.14
  47.0 4.8 %all-to-all-start = ((f32[64,32,256]{2,1,0:T(8,128)}), f32[64,32,256]{2,1,0:T(8,128)S(1)}, u32[]{:S(2)}, u32[]{:S(2)}) async-start(f32[64,32,256]{2,1,0:T(8,128)} %broadcast_in_dim.14), calls=%async_computation | async-start | bytes 4194304 | tf_op jit(solution)/shard_map/all_to_all | solution.py:14
  51.8 0.8 reshape.41.g_ref
  52.6 42.6 %shard_map.41 = f32[256,256]{1,0:T(8,128)} custom-call(f32[256,256]{1,0:T(8,128)} %reshape.41.g_ref), custom_call_target="tpu_custom_call" | custom-call | flops 33554432 | bytes 524288 | tf_op jit(solution)/shard_map/pallas_call | solution.py:74
  95.2 6.3 %all-to-all-done = f32[64,32,256]{2,1,0:T(8,128)S(1)} async-done(((f32[64,32,256]{2,1,0:T(8,128)}), f32[64,32,256]{2,1,0:T(8,128)S(1)}, u32[]{:S(2)}, u32[]{:S(2)}) %all-to-all-start) | async-done | bytes 2097184 | tf_op jit(solution)/shard_map/all_to_all | solution.py:14
  101.5 1.3 copy-done.2
  102.8 3.6 %fusion.13 = f32[2048,256]{1,0:T(8,128)S(1)} fusion(f32[2048,256]{1,0:T(8,128)} %bitcast.32, f32[256,256]{1,0:T(8,128)} %shard_map.41), kind=kOutput, calls=%fused_computation.18 | convolution fusion | flops 1610612736 | bytes 4456448 | tf_op jit(solution)/shard_map/dot_general | solution.py:10
  106.4 2.0 fusion.14
  108.4 19.3 %all_to_all.36 = f32[8,32,256]{2,1,0:T(8,128)S(1)} all-to-all(f32[8,32,256]{2,1,0:T(8,128)S(1)} %bitcast.39), channel_id=1, replica_groups=mesh['row'=64,'col'=8] {'col'}, dimensions={0} | all-to-all | bytes 524288 | tf_op jit(solution)/shard_map/all_to_all | solution.py:14
  128.5 3.4 %all-to-all-start.4 = ((f32[8,32,256]{2,1,0:T(8,128)}), f32[8,32,256]{2,1,0:T(8,128)S(1)}, u32[]{:S(2)}, u32[]{:S(2)}) async-start(f32[8,32,256]{2,1,0:T(8,128)} %broadcast_in_dim.16), calls=%async_computation.4 | async-start | bytes 524288 | tf_op jit(solution)/shard_map/all_to_all | solution.py:14
  132.3 8.9 %all-to-all-done.4 = f32[8,32,256]{2,1,0:T(8,128)S(1)} async-done(((f32[8,32,256]{2,1,0:T(8,128)}), f32[8,32,256]{2,1,0:T(8,128)S(1)}, u32[]{:S(2)}, u32[]{:S(2)}) %all-to-all-start.4) | async-done | bytes 262176 | tf_op jit(solution)/shard_map/all_to_all | solution.py:14
  142.1 70.3 %all_to_all.37 = f32[64,72,128]{2,1,0:T(8,128)S(1)} all-to-all(f32[64,72,128]{2,1,0:T(8,128)S(1)} %pad_maximum_fusion), channel_id=1, replica_groups=mesh['row'=64,'col'=8] {'row'}, dimensions={0} | all-to-all | bytes 4718592 | tf_op jit(solution)/shard_map/all_to_all | solution.py:14
  212.4 1.4 copy-done.1
  214.7 4.7 %all-to-all-start.6 = ((f32[64,4,256]{2,1,0:T(4,128)}), f32[64,4,256]{2,1,0:T(4,128)S(1)}, u32[]{:S(2)}, u32[]{:S(2)}) async-start(f32[64,4,256]{2,1,0:T(4,128)} %broadcast_in_dim.38), calls=%async_computation.6 | async-start | bytes 524288 | tf_op jit(solution)/shard_map/all_to_all | solution.py:14
  219.4 1.7 fusion.11
  221.1 1.9 fusion.5
  223.0 1.9 fusion.7
  224.9 3.6 %fusion.1 = f32[256,2048]{1,0:T(8,128)} fusion(f32[256,2048]{1,0:T(8,128)S(1)} %fusion.5, f32[256,2048]{1,0:T(8,128)S(1)} %fusion.7, f32[256,2048]{1,0:T(8,128)S(1)} %copy-done.4, f32[256,256]{1,0:T(8,128)S(1)} %bitcast.38, f32[2048,256]{1,0:T(8,128)S(1)} %fusion.13), kind=kOutput, calls=%fused_computation.3 | convolution fusion | flops 1612185600 | bytes 10747904 | tf_op jit(solution)/shard_map/dot_general | solution.py:10
  228.5 4.0 %all-to-all-done.6 = f32[64,4,256]{2,1,0:T(4,128)S(1)} async-done(((f32[64,4,256]{2,1,0:T(4,128)}), f32[64,4,256]{2,1,0:T(4,128)S(1)}, u32[]{:S(2)}, u32[]{:S(2)}) %all-to-all-start.6) | async-done | bytes 262176 | tf_op jit(solution)/shard_map/all_to_all | solution.py:14
  233.3 4.8 %convolution_add_fusion = f32[256,2048]{1,0:T(8,128)} fusion(f32[256,2048]{1,0:T(8,128)} %fusion.1, f32[256,256]{1,0:T(8,128)S(1)} %fusion.3, f32[2048,256]{1,0:T(8,128)S(1)} %fusion.13), kind=kOutput, calls=%fused_computation | convolution fusion | flops 1611137024 | bytes 6553600 | tf_op jit(solution)/shard_map/dot_general | solution.py:10
  (31 shorter events, 5.2 us)
Async XLA Ops:
  0.6 1.0 copy-start
  27.6 17.9 %all-to-all-start.2 = ((f32[64,4,256]{2,1,0:T(4,128)}), f32[64,4,256]{2,1,0:T(4,128)S(1)}, u32[]{:S(2)}, u32[]{:S(2)}) async-start(f32[64,4,256]{2,1,0:T(4,128)} %broadcast_in_dim.15), calls=%async_computation.2 | async-start | bytes 524288 | tf_op jit(solution)/shard_map/all_to_all | solution.py:14
  47.0 54.5 %all-to-all-start = ((f32[64,32,256]{2,1,0:T(8,128)}), f32[64,32,256]{2,1,0:T(8,128)S(1)}, u32[]{:S(2)}, u32[]{:S(2)}) async-start(f32[64,32,256]{2,1,0:T(8,128)} %broadcast_in_dim.14), calls=%async_computation | async-start | bytes 4194304 | tf_op jit(solution)/shard_map/all_to_all | solution.py:14
  101.5 1.3 copy-start.2
  102.8 3.6 %copy-start.3 = (f32[256,2048]{1,0:T(8,128)S(1)}, f32[256,2048]{1,0:T(8,128)}, u32[]{:S(2)}) copy-start(f32[256,2048]{1,0:T(8,128)} %param.3) | copy-start | bytes 6291460
  106.4 25.5 %copy-start.5 = (f32[256,256]{1,0:T(8,128)S(1)}, f32[256,256]{1,0:T(8,128)}, u32[]{:S(2)}) copy-start(f32[256,256]{1,0:T(8,128)} %shard_map.41) | copy-start | bytes 786436
  128.5 12.8 %all-to-all-start.4 = ((f32[8,32,256]{2,1,0:T(8,128)}), f32[8,32,256]{2,1,0:T(8,128)S(1)}, u32[]{:S(2)}, u32[]{:S(2)}) async-start(f32[8,32,256]{2,1,0:T(8,128)} %broadcast_in_dim.16), calls=%async_computation.4 | async-start | bytes 524288 | tf_op jit(solution)/shard_map/all_to_all | solution.py:14
  212.4 1.4 copy-start.1
  214.7 17.8 %all-to-all-start.6 = ((f32[64,4,256]{2,1,0:T(4,128)}), f32[64,4,256]{2,1,0:T(4,128)S(1)}, u32[]{:S(2)}, u32[]{:S(2)}) async-start(f32[64,4,256]{2,1,0:T(4,128)} %broadcast_in_dim.38), calls=%async_computation.6 | async-start | bytes 524288 | tf_op jit(solution)/shard_map/all_to_all | solution.py:14
  223.0 1.9 copy-start.4
  232.6 5.6 %copy-start.6 = (f32[256,256]{1,0:T(8,128)}, f32[256,256]{1,0:T(8,128)S(1)}, u32[]{:S(2)}) copy-start(f32[256,256]{1,0:T(8,128)S(1)} %reshape.48) | copy-start | bytes 786436
